TPU v7x, 512 devices: a whole 4x4x16 slice. The times are simulated.
512 devices in a mesh: row: 64 (over z, x), rep: 8 (over y, core).
Axes of the slice: x: 4, y: 4, z: 16, core: 2. Of those that a mesh axis runs over, the one named last changes fastest.
Arguments:
- features: bfloat16 [16384, 128], P('row', 'rep'), may hold values from -6 to 6
- owner_index: int32 [16384], P('row'), may hold values from 0 to 16383, as said below
- block_cols: int32 [128, 64], P('row', 'rep'), may hold values from 0 to 127, as said below
- block_count: int32 [128], P('row'), may hold values from 1 to 64, as said below
- tiles: bfloat16 [128, 64, 128, 128], P('row', 'rep'), may hold values from -0.109375 to 0.109375
- weight: bfloat16 [128, 256], P(None, 'rep'), may hold values from -0.75 to 0.75
- bias: float32 [256], P('rep'), may hold values from -4 to 4
- grad_out: bfloat16 [16384, 256], P('row', 'rep'), may hold values from -6 to 6
Outputs:
- hidden: bfloat16 [16384, 256], P('row', 'rep')
- weight_grad: float32 [128, 256], P(None, 'rep')
- bias_grad: float32 [256], P('rep')
Inputs may be any that keep to these rules, and one draw needn't show every extreme that they name: `owner_index`: A permutation; the 256 rows of each loader shard hold exactly 4 positions of every partition's 2*128 rows. `block_cols`: the block columns of one block row are distinct. Block column c belongs to partition c // 2. Over all slots of one partition's 2 block rows, exactly 1 distinct block columns of each partition are named. `block_count`: some block row has all 64 slots live.
All inputs are finite; a program needn't handle non-finite values.
Results may differ from a plain program's by a relative error of at most 0.017.
Values may be sent and summed in bfloat16 or wider, within the bound.
No kernel may reach another device: no remote copies, remote signals or barrier semaphores. Data moves between devices by JAX's collectives and lax.ppermute only.
A program may use at most 64 MiB of HBM per device.

v0:
```python
import jax
import jax.numpy as jnp
from jax import lax
from jax.sharding import PartitionSpec as P


def block_product(tile_set, col_set, live, table, rows_part):
    size_blk = tile_set.shape[2]
    width = table.shape[1]
    blocks = table.reshape(table.shape[0] // size_blk, size_blk, width)
    picked = blocks[col_set]
    picked = jnp.where(live[:, :, None, None], picked, jnp.zeros_like(picked))
    summed = jnp.einsum("rkij,rkjc->ric", tile_set, picked, preferred_element_type=jnp.float32)
    return summed.reshape(rows_part, width)


def on_device(features, owner_index, block_cols, block_count, tiles, weight, bias, grad_out):
    rows_part = features.shape[0]
    cols_dev = features.shape[1]
    parts_count = lax.axis_size("row")
    per_pair = rows_part // parts_count
    destination = owner_index // rows_part
    order = jnp.argsort(destination, stable=True)
    send_rows = features[order].reshape(parts_count, per_pair, cols_dev)
    send_pos = (owner_index[order] % rows_part).reshape(parts_count, per_pair)
    got_rows, got_pos = (
        lax.all_to_all(send_rows, "row", split_axis=0, concat_axis=0, tiled=True),
        lax.all_to_all(send_pos, "row", split_axis=0, concat_axis=0, tiled=True),
    )
    owned = (
        jnp.zeros((rows_part, cols_dev), jnp.bfloat16)
        .at[got_pos.reshape(rows_part)]
        .set(got_rows.reshape(rows_part, cols_dev))
    )
    wide_own = lax.all_gather(owned, "rep", axis=1, tiled=True)
    table = lax.all_gather(wide_own, "row", axis=0, tiled=True)
    slots_dev = block_cols.shape[1]
    slot_ids = lax.axis_index("rep") * slots_dev + jnp.arange(slots_dev, dtype=jnp.int32)
    live = slot_ids[None, :] < block_count[:, None]
    partial_agg = block_product(tiles, block_cols, live, table, rows_part)
    agg = lax.psum(partial_agg.astype(jnp.bfloat16), "rep")
    pre = jnp.dot(agg, weight, preferred_element_type=jnp.float32) + bias
    hidden = jax.nn.silu(pre).astype(jnp.bfloat16)
    sig = jax.nn.sigmoid(pre)
    dpre = (grad_out.astype(jnp.float32) * sig * (1.0 + pre * (1.0 - sig))).astype(jnp.bfloat16)
    weight_term = jnp.dot(agg.T, dpre, preferred_element_type=jnp.float32)
    bias_term = jnp.sum(dpre.astype(jnp.float32), axis=0)
    weight_grad, bias_grad = lax.psum((weight_term, bias_term), "row")
    return (hidden, weight_grad, bias_grad)


def solution(mesh):
    placed = (
        P("row", "rep"),
        P("row"),
        P("row", "rep"),
        P("row"),
        P("row", "rep", None, None),
        P(None, "rep"),
        P("rep"),
        P("row", "rep"),
    )
    return jax.shard_map(
        on_device,
        mesh=mesh,
        in_specs=placed,
        out_specs=(P("row", "rep"), P(None, "rep"), P("rep")),
        check_vma=False,
    )
```

profile of v0, /device:TPU:8, one launch (start us, length us, event | category | flops | bytes accessed | tf_op | source)
XLA Modules:
  0.0 583.7 jit_solution(2200357898452502559)
XLA Ops:
  7.2 0.0 copy-start
  7.2 0.7 and_select_fusion
  7.9 3.2 sort.17
  11.1 2.0 gather_fusion
  13.1 0.1 gather.12
  13.2 0.6 add_select_fusion
  13.8 18.6 %all-to-all-start = ((s32[64,1,4]{2,1,0:T(1,128)}), s32[64,1,4]{2,1,0:T(1,128)S(1)}, u32[]{:S(2)}, u32[]{:S(2)}) async-start(s32[64,1,4]{2,1,0:T(1,128)} %bitcast), calls=%async_computation | async-start | bytes 65536 | tf_op jit(solution)/shard_map/all_to_all | solution.py:28
  32.4 0.8 copy.18
  33.2 1.5 gather_fusion.1
  34.7 12.5 %all-to-all-done = s32[64,1,4]{2,1,0:T(1,128)S(1)} async-done(((s32[64,1,4]{2,1,0:T(1,128)}), s32[64,1,4]{2,1,0:T(1,128)S(1)}, u32[]{:S(2)}, u32[]{:S(2)}) %all-to-all-start) | async-done | bytes 1056 | tf_op jit(solution)/shard_map/all_to_all | solution.py:28
  47.2 4.6 all-to-all-start.1
  51.8 0.0 all-gather.2.cloned.1.call-start
  51.8 0.5 broadcast.122
  52.3 0.7 reduce.3
  53.1 0.1 reshape.138
  53.2 13.9 %all-to-all-done.1 = bf16[64,4,16]{2,1,0:T(4,128)(2,1)S(1)} async-done(((bf16[64,4,16]{2,1,0:T(4,128)(2,1)}), bf16[64,4,16]{2,1,0:T(4,128)(2,1)S(1)}, u32[]{:S(2)}, u32[]{:S(2)}) %all-to-all-start.1) | async-done | bytes 8224 | tf_op jit(solution)/shard_map/all_to_all | solution.py:27
  67.1 1.2 scatter_custom_fusion
  68.2 0.1 copy.19
  68.3 14.0 %all_gather.6 = bf16[256,128]{0,1:T(8,128)(2,1)} all-gather(bf16[256,16]{0,1:T(8,128)(2,1)S(1)} %copy.19), channel_id=1, replica_groups=mesh['row'=64,'rep'=8] {'rep'}, dimensions={1}, use_global_device_ids=true | all-gather | bytes 73728 | tf_op jit(solution)/shard_map/all_gather | solution.py:35
  82.3 0.0 all-gather.2.cloned.1.call-update
  82.4 0.0 all-reduce.3.cloned.1.call-start
  82.4 0.7 compare_select_fusion.1
  83.1 0.1 reshape.160
  83.2 0.7 broadcast_compare_fusion
  83.9 0.0 copy-start.1
  83.9 0.0 copy-start.2
  83.9 0.0 copy-start.3
  83.9 133.4 %all-gather.2.cloned.1.call-done = bf16[16384,128]{0,1:T(8,128)(2,1)} async-done(((bf16[256,128]{0,1:T(8,128)(2,1)}), bf16[16384,128]{0,1:T(8,128)(2,1)}) %all-gather.2.cloned.1.call-update) | async-done | bytes 4194320 | tf_op jit(solution)/shard_map/all_gather | solution.py:36
  217.4 6.4 %copy.20 = bf16[16384,128]{1,0:T(8,128)(2,1)} copy(bf16[16384,128]{0,1:T(8,128)(2,1)} %all-gather.2.cloned.1.call-done) | data formatting | bytes 8388608 | tf_op jit(solution)/shard_map/all_gather | solution.py:36
  223.7 2.8 gather_fusion.2
  226.6 0.0 copy-done
  226.6 1.0 fusion
  227.6 0.0 all-reduce.3.cloned.1.call-update
  227.6 66.4 %all-reduce.3.cloned.1.call-done = bf16[256,128]{1,0:T(8,128)(2,1)} async-done(((bf16[256,128]{1,0:T(8,128)(2,1)}), bf16[256,128]{1,0:T(8,128)(2,1)}) %all-reduce.3.cloned.1.call-update) | async-done | bytes 65552 | tf_op jit(solution)/shard_map/psum | solution.py:41
  294.0 0.0 copy-done.1
  294.0 0.0 copy-done.2
  294.0 0.0 copy-done.3
  294.0 1.7 convert_reduce_fusion
  295.8 1.0 fusion.8
  296.7 280.1 %all-reduce = (f32[128,32]{0,1:T(8,128)}, f32[32]{0:T(128)}) all-reduce(f32[128,32]{0,1:T(8,128)S(1)} %fusion.8, f32[32]{0:T(128)S(1)} %get-tuple-element.7), channel_id=1, replica_groups=mesh['row'=64,'rep'=8] {'row'}, use_global_device_ids=true, to_apply=%region_3.4 | all-reduce | flops 4128 | bytes 33024 | tf_op jit(solution)/shard_map/psum | solution.py:48
  (6 shorter events, 0.0 us)
Async XLA Ops:
  7.2 219.4 %copy-start = (bf16[2,8,128,128]{3,2,1,0:T(8,128)(2,1)S(1)}, bf16[2,8,128,128]{3,2,1,0:T(8,128)(2,1)}, u32[]{:S(2)}) copy-start(bf16[2,8,128,128]{3,2,1,0:T(8,128)(2,1)} %param.12) | copy-start | bytes 1572868
  13.8 33.3 %all-to-all-start = ((s32[64,1,4]{2,1,0:T(1,128)}), s32[64,1,4]{2,1,0:T(1,128)S(1)}, u32[]{:S(2)}, u32[]{:S(2)}) async-start(s32[64,1,4]{2,1,0:T(1,128)} %bitcast), calls=%async_computation | async-start | bytes 65536 | tf_op jit(solution)/shard_map/all_to_all | solution.py:28
  47.2 19.9 %all-to-all-start.1 = ((bf16[64,4,16]{2,1,0:T(4,128)(2,1)}), bf16[64,4,16]{2,1,0:T(4,128)(2,1)S(1)}, u32[]{:S(2)}, u32[]{:S(2)}) async-start(bf16[64,4,16]{2,1,0:T(4,128)(2,1)} %bitcast.2), calls=%async_computation.1 | async-start | bytes 131072 | tf_op jit(solution)/shard_map/all_to_all | solution.py:27
  51.8 165.6 %all-gather.2.cloned.1.call-start = ((), (), s32[]{:S(2)}) async-start(), calls=%async_computation.2 | async-start | bytes 4259840 | tf_op jit(solution)/shard_map/all_gather | solution.py:36
  82.4 211.7 %all-reduce.3.cloned.1.call-start = ((), (), s32[]{:S(2)}) async-start(), calls=%async_computation.3 | async-start | bytes 131072 | tf_op jit(solution)/shard_map/psum | solution.py:41
  83.9 210.1 %copy-start.1 = (bf16[256,32]{0,1:T(8,128)(2,1)S(1)}, bf16[256,32]{0,1:T(8,128)(2,1)}, u32[]{:S(2)}) copy-start(bf16[256,32]{0,1:T(8,128)(2,1)} %param.15) | copy-start | bytes 49156
  83.9 210.1 %copy-start.2 = (bf16[128,32]{0,1:T(8,128)(2,1)S(1)}, bf16[128,32]{0,1:T(8,128)(2,1)}, u32[]{:S(2)}) copy-start(bf16[128,32]{0,1:T(8,128)(2,1)} %param.13) | copy-start | bytes 24580
  83.9 210.1 %copy-start.3 = (f32[32]{0:T(128)S(1)}, f32[32]{0:T(128)}, u32[]{:S(2)}) copy-start(f32[32]{0:T(128)} %param.14) | copy-start | bytes 388
Sparse Core Ops, SparseCore 0:
  82.5 134.8 all-gather.1
  227.7 66.2 all-reduce.2
where the time goes:
time: 584 us
  blocking collectives  294 us (50%)
  waiting for transfers between devices  226 us (39%)
  starting transfers between devices  23.3 us (4%)
  local copies, waits for them, and re-layouts  15.5 us (3%)
  between operations  14.1 us (2%)
  other arithmetic  6.69 us (1%)
    psum x1, blocking collectives, on_device(): weight_grad, bias_grad = lax.psum((weight_term, bias_term), 'row')  280 us
    all_gather x1, waiting for transfers between devices, on_device(): table = lax.all_gather(wide_own, 'row', axis=0, tiled=True)  133 us
    psum x1, waiting for transfers between devices, on_device(): agg = lax.psum(partial_agg.astype(jnp.bfloat16), 'rep')  66.4 us
    all_to_all x1, starting transfers between devices, on_device(): lax.all_to_all(send_pos, 'row', split_axis=0, concat_axis=0, tiled=True)  18.6 us
    all_gather x1, blocking collectives, on_device(): wide_own = lax.all_gather(owned, 'rep', axis=1, tiled=True)  14 us
    all_to_all x1, waiting for transfers between devices, on_device(): lax.all_to_all(send_rows, 'row', split_axis=0, concat_axis=0, tiled=True)  13.9 us
    all_to_all x1, waiting for transfers between devices, on_device(): lax.all_to_all(send_pos, 'row', split_axis=0, concat_axis=0, tiled=True)  12.5 us
  transfers between devices with their start and end apart: 4, of which 4 were waited for; matrix products, arithmetic and copies ran while one was open for 1% of the time, Pallas kernels for 0%

commit v1 on v0

v1 whole, which is shorter than its diff:
```python
import jax
import jax.numpy as jnp
from jax import lax
from jax.sharding import PartitionSpec as P


def sum_over(x, axis_name, count):
    rows = x.shape[0]
    pieces = x.reshape((count, rows // count) + x.shape[1:])
    got = lax.all_to_all(pieces, axis_name, 0, 0, tiled=True)
    reduced = jnp.sum(got.astype(jnp.float32), axis=0)
    return reduced


def spread(x, axis_name, count):
    wide = jnp.broadcast_to(x[None], (count,) + x.shape)
    return lax.all_to_all(wide, axis_name, 0, 0, tiled=True)


def on_device(features, owner_index, block_cols, block_count, tiles, weight, bias, grad_out):
    rows_part, cols_dev = features.shape
    parts = lax.axis_size("row")
    reps = lax.axis_size("rep")
    per_pair = rows_part // parts
    rb, slots_dev, size_blk = tiles.shape[0], tiles.shape[1], tiles.shape[2]

    destination = owner_index // rows_part
    order = jnp.argsort(destination, stable=True)
    send_rows = features[order]
    send_pos = (owner_index[order] % rows_part).astype(jnp.bfloat16)
    packet = jnp.concatenate([send_rows.T, send_pos[None, :]], axis=0)
    everyone = spread(packet, "row", parts)
    width = cols_dev + 1
    grouped = everyone.reshape(parts, width, parts, per_pair).transpose(2, 1, 0, 3).reshape(parts, width, rows_part)
    pos = grouped[:, cols_dev, :].astype(jnp.int32)
    values = grouped[:, :cols_dev, :]

    cols_all = lax.all_gather(block_cols, "rep", axis=1, tiled=True)
    part_of = cols_all // rb
    half_of = cols_all % rb
    part_ids = jnp.arange(parts, dtype=jnp.int32)
    hit = part_of[None, :, :] == part_ids[:, None, None]
    half = jnp.max(jnp.where(hit, half_of[None, :, :], 0), axis=(1, 2))
    node_ids = jnp.arange(size_blk, dtype=jnp.int32)
    target = half[:, None, None] * size_blk + node_ids[None, None, :]
    pick = (pos[:, :, None] == target).astype(jnp.bfloat16)
    needed = jnp.einsum("qfg,qgn->qfn", values, pick, preferred_element_type=jnp.float32).astype(jnp.bfloat16)

    peer_parts = part_of.reshape(rb, reps, slots_dev).transpose(1, 0, 2)
    outgoing = needed[peer_parts]
    incoming = lax.all_to_all(outgoing, "rep", 0, 0, tiled=True)

    slot_ids = lax.axis_index("rep") * slots_dev + jnp.arange(slots_dev, dtype=jnp.int32)
    live = slot_ids[None, :] < block_count[:, None]
    tiles_live = jnp.where(live[:, :, None, None], tiles, jnp.zeros_like(tiles))
    partial = jnp.einsum("rsin,jrsfn->rijf", tiles_live, incoming, preferred_element_type=jnp.float32)
    partial = partial.reshape(rows_part, reps * cols_dev)

    agg_part = sum_over(partial, "rep", reps).astype(jnp.bfloat16)
    agg = spread(agg_part, "rep", reps).reshape(rows_part, reps * cols_dev)

    pre = jnp.dot(agg, weight, preferred_element_type=jnp.float32) + bias
    hidden = jax.nn.silu(pre).astype(jnp.bfloat16)
    sig = jax.nn.sigmoid(pre)
    dpre = (grad_out.astype(jnp.float32) * sig * (1.0 + pre * (1.0 - sig))).astype(jnp.bfloat16)
    weight_term = jnp.dot(agg.T, dpre, preferred_element_type=jnp.float32)
    bias_term = jnp.sum(dpre.astype(jnp.float32), axis=0)

    flat = jnp.concatenate([weight_term.reshape(-1), bias_term])
    lanes = 128
    chunk = lanes * (-(-flat.shape[0] // (parts * lanes)))
    flat = jnp.pad(flat, (0, parts * chunk - flat.shape[0])).reshape(parts, chunk)
    total = spread(sum_over(flat, "row", parts), "row", parts).reshape(-1)
    n_w = weight_term.size
    weight_grad = total[:n_w].reshape(weight_term.shape)
    bias_grad = total[n_w:n_w + bias_term.shape[0]]
    return (hidden, weight_grad, bias_grad)


def solution(mesh):
    placed = (
        P("row", "rep"),
        P("row"),
        P("row", "rep"),
        P("row"),
        P("row", "rep", None, None),
        P(None, "rep"),
        P("rep"),
        P("row", "rep"),
    )
    return jax.shard_map(
        on_device,
        mesh=mesh,
        in_specs=placed,
        out_specs=(P("row", "rep"), P(None, "rep"), P("rep")),
        check_vma=False,
    )
```

time: 584 us -> 154 us (0.26)
  blocking collectives: 294 us -> 64.1 us
  waiting for transfers between devices: 226 us -> 43.6 us
  between operations: 14.1 us -> 0.84 us
    psum x1 -> x0, blocking collectives: 280 us -> none  [on_device(): weight_grad, bias_grad = lax.psum((weight_term, bias_term), 'row')]
    all_gather x1 -> x0, waiting for transfers between devices: 133 us -> none  [on_device(): table = lax.all_gather(wide_own, 'row', axis=0, tiled=True)]
    psum x1 -> x0, waiting for transfers between devices: 66.4 us -> none  [on_device(): agg = lax.psum(partial_agg.astype(jnp.bfloat16), 'rep')]
    all_to_all x0 -> x4, blocking collectives: none -> 55.3 us  [the longest x2 28.8 us: sum_over(): got = lax.all_to_all(pieces, axis_name, 0, 0, tiled=True)]
    all_to_all x2, waiting for transfers between devices: 26.4 us -> 43.6 us  [the longest x1 34.8 us: spread(): return lax.all_to_all(wide, axis_name, 0, 0, tiled=True)]
    all_gather x1, local copies, waits for them, and re-layouts: 6.37 us -> 0.01 us  [on_device(): cols_all = lax.all_gather(block_cols, 'rep', axis=1, tiled=True)]
  transfers between devices with their start and end apart: 4 -> 2, of which waited for: 4 -> 2; matrix products, arithmetic and copies ran while one was open for 1% -> 0% of each run, Pallas kernels for 0% -> 0%
where the time goes in v1:
time: 154 us; the launch traced here: 153 us
  blocking collectives  64.1 us (42%)
  waiting for transfers between devices  43.6 us (28%)
  starting transfers between devices  23.5 us (15%)
  local copies, waits for them, and re-layouts  11.9 us (8%)
  matrix products  5.13 us (3%)
  other arithmetic  4.26 us (3%)
    all_to_all x1, waiting for transfers between devices, spread(): return lax.all_to_all(wide, axis_name, 0, 0, tiled=True)  34.8 us
    all_to_all x2, blocking collectives, sum_over(): got = lax.all_to_all(pieces, axis_name, 0, 0, tiled=True)  28.8 us
    all_to_all x2, blocking collectives, spread(): return lax.all_to_all(wide, axis_name, 0, 0, tiled=True)  26.5 us
    all_to_all x1, starting transfers between devices, spread(): return lax.all_to_all(wide, axis_name, 0, 0, tiled=True)  18.6 us
    all_to_all x1, waiting for transfers between devices, on_device(): incoming = lax.all_to_all(outgoing, 'rep', 0, 0, tiled=True)  8.81 us
    all_gather x1, blocking collectives, on_device(): cols_all = lax.all_gather(block_cols, 'rep', axis=1, tiled=True)  8.77 us
    all_to_all x1, starting transfers between devices, on_device(): incoming = lax.all_to_all(outgoing, 'rep', 0, 0, tiled=True)  4.92 us
    dot_general x1, matrix products, on_device(): jnp.einsum('qfg,qgn->qfn', values, pick, preferred_element_type=jnp.float32)  3.69 us
  transfers between devices with their start and end apart: 2, of which 2 were waited for; matrix products, arithmetic and copies ran while one was open for 0% of the time, Pallas kernels for 0%

profile of v1, /device:TPU:8, one launch (start us, length us, event | category | flops | bytes accessed | tf_op | source)
XLA Modules:
  0.0 153.3 jit_solution(980085118121361113)
XLA Ops:
  0.6 0.0 copy-start
  0.6 0.7 and_select_fusion.3
  1.3 3.2 %sort.17 = (s32[256]{0:T(256)}, s32[256]{0:T(256)S(1)}) sort(s32[256]{0:T(256)S(1)} %and_select_fusion.3, s32[256]{0:T(256)S(1)} %iota.22), dimensions={0}, to_apply=%region_0.1 | sort | flops 2048 | bytes 4096 | tf_op jit(solution)/shard_map/jit(argsort)/sort | solution.py:28
  4.5 2.0 %gather_fusion.1 = s32[256]{0:T(256)S(1)} fusion(s32[256]{0:T(256)} %param.9, s32[1024]{0:T(1024)S(1)} %pad_clamp_fusion.1), kind=kCustom, calls=%fused_computation.1 | custom fusion | bytes 3072 | tf_op jit(solution)/shard_map/gather | solution.py:30
  6.5 0.8 copy.76
  7.3 0.9 gather_fusion
  8.2 0.1 copy.77
  8.3 0.0 copy-start.1
  8.3 0.9 broadcast_in_dim.35
  9.2 18.6 %all-to-all-start = ((bf16[64,17,256]{2,1,0:T(8,128)(2,1)}), bf16[64,17,256]{2,1,0:T(8,128)(2,1)S(1)}, u32[]{:S(2)}, u32[]{:S(2)}) async-start(bf16[64,17,256]{2,1,0:T(8,128)(2,1)} %broadcast_in_dim.35), calls=%async_computation | async-start | bytes 1572864 | tf_op jit(solution)/shard_map/all_to_all | solution.py:17
  27.8 0.0 copy-done.1
  27.8 8.8 %all-gather = s32[8,8,2]{1,2,0:T(2,128)S(1)} all-gather(s32[1,8,2]{1,2,0:T(2,128)S(1)} %bitcast.68), channel_id=1, replica_groups=mesh['row'=64,'rep'=8] {'rep'}, dimensions={0}, use_global_device_ids=true | all-gather | bytes 576 | tf_op jit(solution)/shard_map/all_gather | solution.py:38
  36.6 0.1 reshape.183
  36.7 0.1 reshape.148
  36.8 0.1 reshape.172
  36.9 0.1 select_reduce_fusion
  37.0 0.1 iota_add_fusion
  37.1 34.8 %all-to-all-done = bf16[64,17,256]{2,1,0:T(8,128)(2,1)S(1)} async-done(((bf16[64,17,256]{2,1,0:T(8,128)(2,1)}), bf16[64,17,256]{2,1,0:T(8,128)(2,1)S(1)}, u32[]{:S(2)}, u32[]{:S(2)}) %all-to-all-start) | async-done | bytes 557088 | tf_op jit(solution)/shard_map/all_to_all | solution.py:17
  71.8 0.8 copy.78
  72.7 1.7 %copy.79 = bf16[64,17,64,4]{0,3,2,1:T(4,128)(2,1)S(1)} copy(bf16[64,17,64,4]{2,3,0,1:T(4,128)(2,1)S(1)} %bitcast.60) | data formatting | bytes 1114112 | tf_op jit(solution)/shard_map/transpose | solution.py:34
  74.4 0.1 slice.23
  74.5 0.8 copy.96
  75.4 0.1 copy.81
  75.4 3.7 %fusion.4 = bf16[64,16,128]{2,1,0:T(8,128)(2,1)S(1)} fusion(bf16[64,16,256]{2,1,0:T(8,128)(2,1)S(1)} %copy.96, s32[64,128]{1,0:T(8,128)S(1)} %iota_add_fusion, s32[64,256]{1,0:T(8,128)S(1)} %copy.81), kind=kOutput, calls=%fused_computation.7 | convolution fusion | flops 69337088 | bytes 884736 | tf_op jit(solution)/shard_map/qfg,qgn->qfn/dot_general | solution.py:47
  79.1 0.0 copy-start.4
  79.1 0.0 copy-start.2
  79.1 1.5 gather_fusion.2
  80.6 4.9 %all-to-all-start.1 = ((bf16[8,2,8,16,128]{4,3,2,1,0:T(8,128)(2,1)}), bf16[8,2,8,16,128]{4,3,2,1,0:T(8,128)(2,1)S(1)}, u32[]{:S(2)}, u32[]{:S(2)}) async-start(bf16[8,2,8,16,128]{4,3,2,1,0:T(8,128)(2,1)} %bitcast.12), calls=%async_computation.1 | async-start | bytes 1048576 | tf_op jit(solution)/shard_map/all_to_all | solution.py:51
  85.5 0.0 copy-done.4
  85.6 0.1 broadcast_compare_fusion.1
  85.6 8.8 %all-to-all-done.1 = bf16[8,2,8,16,128]{4,3,2,1,0:T(8,128)(2,1)S(1)} async-done(((bf16[8,2,8,16,128]{4,3,2,1,0:T(8,128)(2,1)}), bf16[8,2,8,16,128]{4,3,2,1,0:T(8,128)(2,1)S(1)}, u32[]{:S(2)}, u32[]{:S(2)}) %all-to-all-start.1) | async-done | bytes 524320 | tf_op jit(solution)/shard_map/all_to_all | solution.py:51
  94.4 0.0 copy-done.2
  94.4 0.4 convolution_bitcast_fusion
  94.8 0.0 copy-start.3
  94.8 0.0 copy-start.5
  94.8 0.1 copy.85
  95.0 0.2 reshape_reshape.6
  95.2 0.2 copy.86
  95.4 8.5 %all_to_all.30 = f32[8,32,128]{2,1,0:T(8,128)S(1)} all-to-all(f32[8,32,128]{2,1,0:T(8,128)S(1)} %copy.86), channel_id=1, replica_groups=mesh['row'=64,'rep'=8] {'rep'}, dimensions={0} | all-to-all | bytes 262144 | tf_op jit(solution)/shard_map/all_to_all | solution.py:10
  103.9 8.0 %all_to_all.31 = bf16[8,32,128]{2,1,0:T(8,128)(2,1)S(1)} all-to-all(bf16[8,32,128]{2,1,0:T(8,128)(2,1)S(1)} %broadcast_in_dim.39), channel_id=1, replica_groups=mesh['row'=64,'rep'=8] {'rep'}, dimensions={0} | all-to-all | bytes 131072 | tf_op jit(solution)/shard_map/all_to_all | solution.py:17
  111.9 0.0 copy-done
  111.9 0.0 copy-done.3
  111.9 0.0 copy-done.5
  112.0 0.9 convert_reduce_fusion
  112.8 0.2 fusion.16
  113.0 0.1 reshape.150
  113.1 20.2 %all_to_all.32 = f32[64,1,128]{2,1,0:T(1,128)S(1)} all-to-all(f32[64,1,128]{2,1,0:T(1,128)S(1)} %bitcast.64), channel_id=1, replica_groups=mesh['row'=64,'rep'=8] {'row'}, dimensions={0} | all-to-all | bytes 65536 | tf_op jit(solution)/shard_map/all_to_all | solution.py:10
  133.4 18.6 %all_to_all.33 = f32[64,1,128]{2,1,0:T(1,128)S(1)} all-to-all(f32[64,1,128]{2,1,0:T(1,128)S(1)} %broadcast_in_dim.40), channel_id=1, replica_groups=mesh['row'=64,'rep'=8] {'row'}, dimensions={0} | all-to-all | bytes 65536 | tf_op jit(solution)/shard_map/all_to_all | solution.py:17
  152.0 0.5 slice.26
  152.5 0.1 reshape.151
  152.6 0.7 copy.91
  (19 shorter events, 0.2 us)
Async XLA Ops:
  0.6 111.3 %copy-start = (bf16[128,32]{0,1:T(8,128)(2,1)S(1)}, bf16[128,32]{0,1:T(8,128)(2,1)}, u32[]{:S(2)}) copy-start(bf16[128,32]{0,1:T(8,128)(2,1)} %param.13) | copy-start | bytes 24580
  8.3 19.5 %copy-start.1 = (s32[2,8]{1,0:T(2,128)S(1)}, s32[2,8]{1,0:T(2,128)}, u32[]{:S(2)}) copy-start(s32[2,8]{1,0:T(2,128)} %param.10) | copy-start | bytes 196
  9.2 62.6 %all-to-all-start = ((bf16[64,17,256]{2,1,0:T(8,128)(2,1)}), bf16[64,17,256]{2,1,0:T(8,128)(2,1)S(1)}, u32[]{:S(2)}, u32[]{:S(2)}) async-start(bf16[64,17,256]{2,1,0:T(8,128)(2,1)} %broadcast_in_dim.35), calls=%async_computation | async-start | bytes 1572864 | tf_op jit(solution)/shard_map/all_to_all | solution.py:17
  79.1 6.4 %copy-start.4 = (s32[2]{0:T(128)S(1)}, s32[2]{0:T(128)}, u32[]{:S(2)}) copy-start(s32[2]{0:T(128)} %param.11) | copy-start | bytes 28
  79.1 15.3 %copy-start.2 = (bf16[2,8,128,128]{3,2,1,0:T(8,128)(2,1)S(1)}, bf16[2,8,128,128]{3,2,1,0:T(8,128)(2,1)}, u32[]{:S(2)}) copy-start(bf16[2,8,128,128]{3,2,1,0:T(8,128)(2,1)} %param.12) | copy-start | bytes 1572868
  80.6 13.8 %all-to-all-start.1 = ((bf16[8,2,8,16,128]{4,3,2,1,0:T(8,128)(2,1)}), bf16[8,2,8,16,128]{4,3,2,1,0:T(8,128)(2,1)S(1)}, u32[]{:S(2)}, u32[]{:S(2)}) async-start(bf16[8,2,8,16,128]{4,3,2,1,0:T(8,128)(2,1)} %bitcast.12), calls=%async_computation.1 | async-start | bytes 1048576 | tf_op jit(solution)/shard_map/all_to_all | solution.py:51
  94.8 17.1 %copy-start.3 = (bf16[256,32]{0,1:T(8,128)(2,1)S(1)}, bf16[256,32]{0,1:T(8,128)(2,1)}, u32[]{:S(2)}) copy-start(bf16[256,32]{0,1:T(8,128)(2,1)} %param.15) | copy-start | bytes 49156
  94.8 17.1 %copy-start.5 = (f32[32]{0:T(128)S(1)}, f32[32]{0:T(128)}, u32[]{:S(2)}) copy-start(f32[32]{0:T(128)} %param.14) | copy-start | bytes 388

commit v2 on v1

--- a/solution.py
+++ b/solution.py
@@ -25,15 +25,20 @@
     rb, slots_dev, size_blk = tiles.shape[0], tiles.shape[1], tiles.shape[2]
 
     destination = owner_index // rows_part
-    order = jnp.argsort(destination, stable=True)
-    send_rows = features[order]
-    send_pos = (owner_index[order] % rows_part).astype(jnp.bfloat16)
-    packet = jnp.concatenate([send_rows.T, send_pos[None, :]], axis=0)
-    everyone = spread(packet, "row", parts)
+    same = destination[:, None] == destination[None, :]
+    before = jnp.arange(rows_part)[:, None] > jnp.arange(rows_part)[None, :]
+    rank = jnp.sum(same & before, axis=1)
+    slot = destination * per_pair + rank
+    place = (slot[:, None] == jnp.arange(rows_part)[None, :]).astype(jnp.bfloat16)
+    pos_row = (owner_index % rows_part).astype(jnp.bfloat16)
+    loader = jnp.concatenate([features.T, pos_row[None, :]], axis=0)
+    packet = jnp.dot(loader, place, preferred_element_type=jnp.float32).astype(jnp.bfloat16)
     width = cols_dev + 1
-    grouped = everyone.reshape(parts, width, parts, per_pair).transpose(2, 1, 0, 3).reshape(parts, width, rows_part)
-    pos = grouped[:, cols_dev, :].astype(jnp.int32)
-    values = grouped[:, :cols_dev, :]
+    packet = packet.reshape(width, parts, per_pair)
+    wide = jnp.broadcast_to(packet[None], (parts,) + packet.shape)
+    grouped = lax.all_to_all(wide, "row", 0, 3, tiled=True).reshape(width, parts, rows_part)
+    pos = grouped[cols_dev].astype(jnp.int32)
+    values = grouped[:cols_dev]
 
     cols_all = lax.all_gather(block_cols, "rep", axis=1, tiled=True)
     part_of = cols_all // rb
@@ -44,7 +49,7 @@
     node_ids = jnp.arange(size_blk, dtype=jnp.int32)
     target = half[:, None, None] * size_blk + node_ids[None, None, :]
     pick = (pos[:, :, None] == target).astype(jnp.bfloat16)
-    needed = jnp.einsum("qfg,qgn->qfn", values, pick, preferred_element_type=jnp.float32).astype(jnp.bfloat16)
+    needed = jnp.einsum("fqg,qgn->qfn", values, pick, preferred_element_type=jnp.float32).astype(jnp.bfloat16)
 
     peer_parts = part_of.reshape(rb, reps, slots_dev).transpose(1, 0, 2)
     outgoing = needed[peer_parts]
@@ -56,8 +61,8 @@
     partial = jnp.einsum("rsin,jrsfn->rijf", tiles_live, incoming, preferred_element_type=jnp.float32)
     partial = partial.reshape(rows_part, reps * cols_dev)
 
-    agg_part = sum_over(partial, "rep", reps).astype(jnp.bfloat16)
-    agg = spread(agg_part, "rep", reps).reshape(rows_part, reps * cols_dev)
+    shares = spread(partial.astype(jnp.bfloat16), "rep", reps)
+    agg = jnp.sum(shares.astype(jnp.float32), axis=0).astype(jnp.bfloat16)
 
     pre = jnp.dot(agg, weight, preferred_element_type=jnp.float32) + bias
     hidden = jax.nn.silu(pre).astype(jnp.bfloat16)

time: 154 us -> 135 us (0.88)
  waiting for transfers between devices: 43.6 us -> 33.7 us
  blocking collectives: 64.1 us -> 60.3 us
  other arithmetic: 4.26 us -> 1.3 us
  local copies, waits for them, and re-layouts: 11.9 us -> 9.11 us
    all_to_all x1, waiting for transfers between devices: 34.8 us -> 24.9 us  [on_device(): lax.all_to_all(wide, 'row', 0, 3, tiled=True)]
    all_to_all x2 -> x1, blocking collectives: 28.8 us -> 20.2 us  [sum_over(): got = lax.all_to_all(pieces, axis_name, 0, 0, tiled=True)]
    all_to_all x2, blocking collectives: 26.5 us -> 31.3 us  [spread(): return lax.all_to_all(wide, axis_name, 0, 0, tiled=True)]
    sort x1 -> x0, other arithmetic: 3.17 us -> none  [on_device(): order = jnp.argsort(destination, stable=True)]
    gather x2 -> x0, local copies, waits for them, and re-layouts: 2.84 us -> none  [the longest x1 1.98 us: on_device(): send_pos = (owner_index[order] % rows_part).astype(jnp.bfloat16)]
    slice x1 -> x5, local copies, waits for them, and re-layouts: 0.09 us -> 2.18 us  [the longest x3 2.18 us: on_device(): values = grouped[:cols_dev]]
    transpose x2 -> x0, local copies, waits for them, and re-layouts: 1.78 us -> none  [the longest x1 1.71 us: on_device(): everyone.reshape(parts, width, parts, per_pair).transpose(2, 1, 0, 3)]
    unnamed x16 -> x20, local copies, waits for them, and re-layouts: 2.47 us -> 3.54 us
where the time goes in v2:
time: 135 us
  blocking collectives  60.3 us (45%)
  waiting for transfers between devices  33.7 us (25%)
  starting transfers between devices  23.5 us (17%)
  local copies, waits for them, and re-layouts  9.11 us (7%)
  matrix products  6.06 us (4%)
    all_to_all x2, blocking collectives, spread(): return lax.all_to_all(wide, axis_name, 0, 0, tiled=True)  31.3 us
    all_to_all x1, waiting for transfers between devices, on_device(): lax.all_to_all(wide, 'row', 0, 3, tiled=True)  24.9 us
    all_to_all x1, blocking collectives, sum_over(): got = lax.all_to_all(pieces, axis_name, 0, 0, tiled=True)  20.2 us
    all_to_all x1, starting transfers between devices, on_device(): lax.all_to_all(wide, 'row', 0, 3, tiled=True)  18.6 us
    all_to_all x1, waiting for transfers between devices, on_device(): incoming = lax.all_to_all(outgoing, 'rep', 0, 0, tiled=True)  8.81 us
    all_gather x1, blocking collectives, on_device(): cols_all = lax.all_gather(block_cols, 'rep', axis=1, tiled=True)  8.77 us
    all_to_all x1, starting transfers between devices, on_device(): incoming = lax.all_to_all(outgoing, 'rep', 0, 0, tiled=True)  4.92 us
    dot_general x1, matrix products, on_device(): jnp.einsum('fqg,qgn->qfn', values, pick, preferred_element_type=jnp.float32)  3.69 us
  transfers between devices with their start and end apart: 2, of which 2 were waited for; matrix products, arithmetic and copies ran while one was open for 0% of the time, Pallas kernels for 0%

profile of v2, /device:TPU:8, one launch (start us, length us, event | category | flops | bytes accessed | tf_op | source)
XLA Modules:
  0.0 134.9 jit_solution(9720771332290993717)
XLA Ops:
  0.6 0.0 copy-start
  0.6 0.7 fusion.18
  1.3 0.2 convert_reduce_fusion
  1.5 0.9 convolution_convert_fusion
  2.5 0.1 copy.51
  2.6 0.1 copy.52
  2.7 0.3 broadcast_bitcast_fusion
  3.0 0.0 copy-start.2
  3.0 1.6 %reshape.135 = bf16[64,2,2176]{2,1,0:T(2,128)(2,1)} reshape(bf16[64,17,4,64]{3,2,1,0:T(4,128)(2,1)S(1)} %broadcast_bitcast_fusion) | data formatting | bytes 1114112
  4.6 18.6 %all-to-all-start = ((bf16[64,2,2176]{2,1,0:T(2,128)(2,1)}), bf16[64,2,2176]{2,1,0:T(2,128)(2,1)S(1)}, u32[]{:S(2)}, u32[]{:S(2)}) async-start(bf16[64,2,2176]{2,1,0:T(2,128)(2,1)} %reshape.135), calls=%async_computation | async-start | bytes 1114112 | tf_op jit(solution)/shard_map/all_to_all | solution.py:39
  23.2 0.0 copy-done.2
  23.2 8.8 %all-gather = s32[8,8,2]{1,2,0:T(2,128)S(1)} all-gather(s32[1,8,2]{1,2,0:T(2,128)S(1)} %bitcast.74), channel_id=1, replica_groups=mesh['row'=64,'rep'=8] {'rep'}, dimensions={0}, use_global_device_ids=true | all-gather | bytes 576 | tf_op jit(solution)/shard_map/all_gather | solution.py:43
  32.0 0.1 reshape.125
  32.1 0.1 reshape.109
  32.2 0.1 reshape.116
  32.3 0.1 select_reduce_fusion
  32.4 0.1 iota_add_fusion
  32.5 24.9 %all-to-all-done = bf16[64,2,2176]{2,1,0:T(2,128)(2,1)S(1)} async-done(((bf16[64,2,2176]{2,1,0:T(2,128)(2,1)}), bf16[64,2,2176]{2,1,0:T(2,128)(2,1)S(1)}, u32[]{:S(2)}, u32[]{:S(2)}) %all-to-all-start) | async-done | bytes 557088 | tf_op jit(solution)/shard_map/all_to_all | solution.py:39
  57.4 0.7 reshape.136
  58.1 0.4 bitcast_bitcast_fusion
  58.5 0.0 copy-start.1
  58.5 0.6 slice.24
  59.1 0.3 copy.53
  59.4 0.1 copy-done.1
  59.5 0.0 slice-start
  59.5 1.3 copy.56
  60.9 0.0 slice-done
  60.9 0.1 copy.54
  61.0 3.7 %fusion.4 = bf16[64,16,128]{2,1,0:T(8,128)(2,1)S(1)} fusion(bf16[16,64,256]{2,0,1:T(8,128)(2,1)S(1)} %copy.56, s32[64,128]{1,0:T(8,128)S(1)} %iota_add_fusion, s32[64,256]{1,0:T(8,128)S(1)} %copy.54), kind=kOutput, calls=%fused_computation.5 | convolution fusion | flops 69337088 | bytes 884736 | tf_op jit(solution)/shard_map/fqg,qgn->qfn/dot_general | solution.py:52
  64.7 0.0 copy-start.5
  64.7 0.0 copy-start.3
  64.7 1.5 %gather_fusion = bf16[128,16,128]{2,1,0:T(8,128)(2,1)} fusion(bf16[64,16,128]{2,1,0:T(8,128)(2,1)S(1)} %fusion.4, s32[1024]{0:T(1024)S(1)} %pad_clamp_fusion), kind=kCustom, calls=%fused_computation | custom fusion | bytes 1049088 | tf_op jit(solution)/shard_map/gather | solution.py:55
  66.2 4.9 %all-to-all-start.1 = ((bf16[8,2,8,16,128]{4,3,2,1,0:T(8,128)(2,1)}), bf16[8,2,8,16,128]{4,3,2,1,0:T(8,128)(2,1)S(1)}, u32[]{:S(2)}, u32[]{:S(2)}) async-start(bf16[8,2,8,16,128]{4,3,2,1,0:T(8,128)(2,1)} %bitcast.13), calls=%async_computation.1 | async-start | bytes 1048576 | tf_op jit(solution)/shard_map/all_to_all | solution.py:56
  71.1 0.0 copy-done.5
  71.1 0.1 broadcast_compare_fusion.3
  71.2 8.8 %all-to-all-done.1 = bf16[8,2,8,16,128]{4,3,2,1,0:T(8,128)(2,1)S(1)} async-done(((bf16[8,2,8,16,128]{4,3,2,1,0:T(8,128)(2,1)}), bf16[8,2,8,16,128]{4,3,2,1,0:T(8,128)(2,1)S(1)}, u32[]{:S(2)}, u32[]{:S(2)}) %all-to-all-start.1) | async-done | bytes 524320 | tf_op jit(solution)/shard_map/all_to_all | solution.py:56
  80.0 0.0 copy-done.3
  80.0 0.4 fusion.7
  80.4 0.1 copy.59
  80.5 0.1 copy.60
  80.6 0.0 copy-start.4
  80.6 0.0 copy-start.6
  80.6 0.1 broadcast_in_dim.42
  80.7 12.8 %all_to_all.35 = bf16[8,256,128]{2,1,0:T(8,128)(2,1)S(1)} all-to-all(bf16[8,256,128]{2,1,0:T(8,128)(2,1)S(1)} %broadcast_in_dim.42), channel_id=1, replica_groups=mesh['row'=64,'rep'=8] {'rep'}, dimensions={0} | all-to-all | bytes 1048576 | tf_op jit(solution)/shard_map/all_to_all | solution.py:17
  93.5 0.1 reduce_sum.40
  93.6 0.0 copy-done
  93.6 0.0 copy-done.4
  93.6 0.0 copy-done.6
  93.6 0.9 convert_reduce_fusion.1
  94.5 0.2 fusion.21
  94.7 0.1 reshape.110
  94.8 20.2 %all_to_all.36 = f32[64,1,128]{2,1,0:T(1,128)S(1)} all-to-all(f32[64,1,128]{2,1,0:T(1,128)S(1)} %bitcast.71), channel_id=1, replica_groups=mesh['row'=64,'rep'=8] {'row'}, dimensions={0} | all-to-all | bytes 65536 | tf_op jit(solution)/shard_map/all_to_all | solution.py:10
  115.1 18.5 %all_to_all.37 = f32[64,1,128]{2,1,0:T(1,128)S(1)} all-to-all(f32[64,1,128]{2,1,0:T(1,128)S(1)} %broadcast_in_dim.43), channel_id=1, replica_groups=mesh['row'=64,'rep'=8] {'row'}, dimensions={0} | all-to-all | bytes 65536 | tf_op jit(solution)/shard_map/all_to_all | solution.py:17
  133.6 0.5 slice.27
  134.1 0.1 reshape.111
  134.2 0.7 copy.63
  (15 shorter events, 0.2 us)
Async XLA Ops:
  0.6 92.9 %copy-start = (bf16[128,32]{0,1:T(8,128)(2,1)S(1)}, bf16[128,32]{0,1:T(8,128)(2,1)}, u32[]{:S(2)}) copy-start(bf16[128,32]{0,1:T(8,128)(2,1)} %param.13) | copy-start | bytes 24580
  3.0 20.2 %copy-start.2 = (s32[2,8]{1,0:T(2,128)S(1)}, s32[2,8]{1,0:T(2,128)}, u32[]{:S(2)}) copy-start(s32[2,8]{1,0:T(2,128)} %param.10) | copy-start | bytes 196
  4.6 52.8 %all-to-all-start = ((bf16[64,2,2176]{2,1,0:T(2,128)(2,1)}), bf16[64,2,2176]{2,1,0:T(2,128)(2,1)S(1)}, u32[]{:S(2)}, u32[]{:S(2)}) async-start(bf16[64,2,2176]{2,1,0:T(2,128)(2,1)} %reshape.135), calls=%async_computation | async-start | bytes 1114112 | tf_op jit(solution)/shard_map/all_to_all | solution.py:39
  58.5 1.0 copy-start.1
  59.5 1.4 %slice-start = ((bf16[1,17,64,64,4]{2,4,1,3,0:T(4,128)(2,1)}), bf16[1,1,64,64,4]{2,4,1,3,0:T(4,128)(2,1)S(1)}, s32[]{:S(2)}) async-start(bf16[1,17,64,64,4]{2,4,1,3,0:T(4,128)(2,1)} %copy-done.1), calls=%async_computation.5 | async-start | bytes 131072 | tf_op jit(solution)/shard_map/slice | solution.py:40
  64.7 6.4 %copy-start.5 = (s32[2]{0:T(128)S(1)}, s32[2]{0:T(128)}, u32[]{:S(2)}) copy-start(s32[2]{0:T(128)} %param.11) | copy-start | bytes 28
  64.7 15.3 %copy-start.3 = (bf16[2,8,128,128]{3,2,1,0:T(8,128)(2,1)S(1)}, bf16[2,8,128,128]{3,2,1,0:T(8,128)(2,1)}, u32[]{:S(2)}) copy-start(bf16[2,8,128,128]{3,2,1,0:T(8,128)(2,1)} %param.12) | copy-start | bytes 1572868
  66.2 13.8 %all-to-all-start.1 = ((bf16[8,2,8,16,128]{4,3,2,1,0:T(8,128)(2,1)}), bf16[8,2,8,16,128]{4,3,2,1,0:T(8,128)(2,1)S(1)}, u32[]{:S(2)}, u32[]{:S(2)}) async-start(bf16[8,2,8,16,128]{4,3,2,1,0:T(8,128)(2,1)} %bitcast.13), calls=%async_computation.1 | async-start | bytes 1048576 | tf_op jit(solution)/shard_map/all_to_all | solution.py:56
  80.6 13.0 %copy-start.4 = (bf16[256,32]{0,1:T(8,128)(2,1)S(1)}, bf16[256,32]{0,1:T(8,128)(2,1)}, u32[]{:S(2)}) copy-start(bf16[256,32]{0,1:T(8,128)(2,1)} %param.15) | copy-start | bytes 49156
  80.6 13.0 %copy-start.6 = (f32[32]{0:T(128)S(1)}, f32[32]{0:T(128)}, u32[]{:S(2)}) copy-start(f32[32]{0:T(128)} %param.14) | copy-start | bytes 388

commit v3 on v2

--- a/solution.py
+++ b/solution.py
@@ -1,7 +1,9 @@
 import jax
 import jax.numpy as jnp
 from jax import lax
-from jax.sharding import PartitionSpec as P
+from jax.sharding import Mesh, PartitionSpec as P
+
+ROW = ("hi", "lo")
 
 
 def sum_over(x, axis_name, count):
@@ -19,7 +21,7 @@
 
 def on_device(features, owner_index, block_cols, block_count, tiles, weight, bias, grad_out):
     rows_part, cols_dev = features.shape
-    parts = lax.axis_size("row")
+    parts = lax.axis_size("hi") * lax.axis_size("lo")
     reps = lax.axis_size("rep")
     per_pair = rows_part // parts
     rb, slots_dev, size_blk = tiles.shape[0], tiles.shape[1], tiles.shape[2]
@@ -35,8 +37,10 @@
     packet = jnp.dot(loader, place, preferred_element_type=jnp.float32).astype(jnp.bfloat16)
     width = cols_dev + 1
     packet = packet.reshape(width, parts, per_pair)
-    wide = jnp.broadcast_to(packet[None], (parts,) + packet.shape)
-    grouped = lax.all_to_all(wide, "row", 0, 3, tiled=True).reshape(width, parts, rows_part)
+    for level in ("lo", "hi"):
+        wide = jnp.broadcast_to(packet[None], (lax.axis_size(level),) + packet.shape)
+        packet = lax.all_to_all(wide, level, 0, 3, tiled=True)[0]
+    grouped = packet
     pos = grouped[cols_dev].astype(jnp.int32)
     values = grouped[:cols_dev]
 
@@ -75,7 +79,7 @@
     lanes = 128
     chunk = lanes * (-(-flat.shape[0] // (parts * lanes)))
     flat = jnp.pad(flat, (0, parts * chunk - flat.shape[0])).reshape(parts, chunk)
-    total = spread(sum_over(flat, "row", parts), "row", parts).reshape(-1)
+    total = spread(sum_over(flat, ROW, parts), ROW, parts).reshape(-1)
     n_w = weight_term.size
     weight_grad = total[:n_w].reshape(weight_term.shape)
     bias_grad = total[n_w:n_w + bias_term.shape[0]]
@@ -83,20 +87,23 @@
 
 
 def solution(mesh):
+    row_size, rep_size = mesh.shape["row"], mesh.shape["rep"]
+    lo_size = 4 if row_size % 4 == 0 else 1
+    split = Mesh(mesh.devices.reshape(row_size // lo_size, lo_size, rep_size), ("hi", "lo", "rep"))
     placed = (
-        P("row", "rep"),
-        P("row"),
-        P("row", "rep"),
-        P("row"),
-        P("row", "rep", None, None),
+        P(ROW, "rep"),
+        P(ROW),
+        P(ROW, "rep"),
+        P(ROW),
+        P(ROW, "rep", None, None),
         P(None, "rep"),
         P("rep"),
-        P("row", "rep"),
+        P(ROW, "rep"),
     )
     return jax.shard_map(
         on_device,
-        mesh=mesh,
+        mesh=split,
         in_specs=placed,
-        out_specs=(P("row", "rep"), P(None, "rep"), P("rep")),
+        out_specs=(P(ROW, "rep"), P(None, "rep"), P("rep")),
         check_vma=False,
     )

time: 135 us -> 138 us (1.022)
  blocking collectives: 60.3 us -> 73.2 us
  waiting for transfers between devices: 33.7 us -> 27.5 us
  starting transfers between devices: 23.5 us -> 20.1 us
    all_to_all x0 -> x1, blocking collectives: none -> 9.55 us  [on_device(): packet = lax.all_to_all(wide, level, 0, 3, tiled=True)[0]]
    all_to_all x1, waiting for transfers between devices: 24.9 us -> 18.6 us  [on_device(): packet = lax.all_to_all(wide, level, 0, 3, tiled=True)[0]]
    all_to_all x1, starting transfers between devices: 18.6 us -> 15.2 us  [on_device(): packet = lax.all_to_all(wide, level, 0, 3, tiled=True)[0]]
    all_to_all x1, blocking collectives: 20.2 us -> 23.5 us  [sum_over(): got = lax.all_to_all(pieces, axis_name, 0, 0, tiled=True)]
    unnamed x20 -> x23, local copies, waits for them, and re-layouts: 3.54 us -> 3.81 us
where the time goes in v3:
time: 138 us; the launch traced here: 137 us
  blocking collectives  73.2 us (53%)
  waiting for transfers between devices  27.5 us (20%)
  starting transfers between devices  20.1 us (15%)
  local copies, waits for them, and re-layouts  8.44 us (6%)
  matrix products  6.05 us (4%)
    all_to_all x2, blocking collectives, spread(): return lax.all_to_all(wide, axis_name, 0, 0, tiled=True)  31.3 us
    all_to_all x1, blocking collectives, sum_over(): got = lax.all_to_all(pieces, axis_name, 0, 0, tiled=True)  23.5 us
    all_to_all x1, waiting for transfers between devices, on_device(): packet = lax.all_to_all(wide, level, 0, 3, tiled=True)[0]  18.6 us
    all_to_all x1, starting transfers between devices, on_device(): packet = lax.all_to_all(wide, level, 0, 3, tiled=True)[0]  15.2 us
    all_to_all x1, blocking collectives, on_device(): packet = lax.all_to_all(wide, level, 0, 3, tiled=True)[0]  9.55 us
    all_to_all x1, waiting for transfers between devices, on_device(): incoming = lax.all_to_all(outgoing, 'rep', 0, 0, tiled=True)  8.81 us
    all_gather x1, blocking collectives, on_device(): cols_all = lax.all_gather(block_cols, 'rep', axis=1, tiled=True)  8.77 us
    all_to_all x1, starting transfers between devices, on_device(): incoming = lax.all_to_all(outgoing, 'rep', 0, 0, tiled=True)  4.92 us
  transfers between devices with their start and end apart: 2, of which 2 were waited for; matrix products, arithmetic and copies ran while one was open for 0% of the time, Pallas kernels for 0%

profile of v3, /device:TPU:8, one launch (start us, length us, event | category | flops | bytes accessed | tf_op | source)
XLA Modules:
  0.0 137.5 jit_solution(11172203246737425074)
XLA Ops:
  0.6 0.0 copy-start
  0.6 0.7 fusion.18
  1.3 0.2 convert_reduce_fusion
  1.5 0.9 convolution_convert_fusion
  2.5 0.1 copy.52
  2.6 0.1 copy.53
  2.8 0.1 reshape.135
  2.9 9.6 %all_to_all.50 = bf16[4,2,2176]{2,1,0:T(2,128)(2,1)S(1)} all-to-all(bf16[4,2,2176]{2,1,0:T(2,128)(2,1)S(1)} %reshape.135), channel_id=1, replica_groups=mesh['hi'=16,'lo'=4,'rep'=8] {'lo'}, dimensions={0} | all-to-all | bytes 69632 | tf_op jit(solution)/shard_map/all_to_all | solution.py:42
  12.4 0.1 reshape.136
  12.6 0.1 broadcast_bitcast_fusion
  12.8 0.0 copy-start.2
  12.8 1.5 %reshape.137 = bf16[16,2,8704]{2,1,0:T(2,128)(2,1)} reshape(bf16[16,17,16,64]{3,2,1,0:T(8,128)(2,1)S(1)} %broadcast_bitcast_fusion) | data formatting | bytes 1114112
  14.3 15.2 %all-to-all-start.1 = ((bf16[16,2,8704]{2,1,0:T(2,128)(2,1)}), bf16[16,2,8704]{2,1,0:T(2,128)(2,1)S(1)}, u32[]{:S(2)}, u32[]{:S(2)}) async-start(bf16[16,2,8704]{2,1,0:T(2,128)(2,1)} %reshape.137), calls=%async_computation.1 | async-start | bytes 1114112 | tf_op jit(solution)/shard_map/all_to_all | solution.py:42
  29.5 0.0 copy-done.2
  29.5 8.8 %all-gather = s32[8,8,2]{1,2,0:T(2,128)S(1)} all-gather(s32[1,8,2]{1,2,0:T(2,128)S(1)} %bitcast.84), channel_id=1, replica_groups=mesh['hi'=16,'lo'=4,'rep'=8] {'rep'}, dimensions={0}, use_global_device_ids=true | all-gather | bytes 576 | tf_op jit(solution)/shard_map/all_gather | solution.py:47
  38.2 0.1 reshape.125
  38.3 0.1 reshape.109
  38.4 0.1 reshape.116
  38.6 0.1 select_reduce_fusion
  38.7 0.1 iota_add_fusion
  38.8 18.6 %all-to-all-done.1 = bf16[16,2,8704]{2,1,0:T(2,128)(2,1)S(1)} async-done(((bf16[16,2,8704]{2,1,0:T(2,128)(2,1)}), bf16[16,2,8704]{2,1,0:T(2,128)(2,1)S(1)}, u32[]{:S(2)}, u32[]{:S(2)}) %all-to-all-start.1) | async-done | bytes 557088 | tf_op jit(solution)/shard_map/all_to_all | solution.py:42
  57.4 0.7 reshape.138
  58.1 0.2 bitcast_bitcast_fusion
  58.3 0.0 copy-start.1
  58.3 0.3 slice.24
  58.6 0.3 copy.55
  58.9 0.4 copy-done.1
  59.3 0.0 slice-start
  59.3 0.8 copy.58
  60.1 0.0 slice-done
  60.2 0.1 copy.56
  60.3 3.7 %fusion.4 = bf16[64,16,128]{2,1,0:T(8,128)(2,1)S(1)} fusion(bf16[16,64,256]{2,0,1:T(8,128)(2,1)S(1)} %copy.58, s32[64,128]{1,0:T(8,128)S(1)} %iota_add_fusion, s32[64,256]{1,0:T(8,128)S(1)} %copy.56), kind=kOutput, calls=%fused_computation.5 | convolution fusion | flops 69337088 | bytes 884736 | tf_op jit(solution)/shard_map/fqg,qgn->qfn/dot_general | solution.py:56
  63.9 0.0 copy-start.5
  63.9 0.0 copy-start.3
  64.0 1.5 %gather_fusion = bf16[128,16,128]{2,1,0:T(8,128)(2,1)} fusion(bf16[64,16,128]{2,1,0:T(8,128)(2,1)S(1)} %fusion.4, s32[1024]{0:T(1024)S(1)} %pad_clamp_fusion), kind=kCustom, calls=%fused_computation | custom fusion | bytes 1049088 | tf_op jit(solution)/shard_map/gather | solution.py:59
  65.4 4.9 %all-to-all-start.2 = ((bf16[8,2,8,16,128]{4,3,2,1,0:T(8,128)(2,1)}), bf16[8,2,8,16,128]{4,3,2,1,0:T(8,128)(2,1)S(1)}, u32[]{:S(2)}, u32[]{:S(2)}) async-start(bf16[8,2,8,16,128]{4,3,2,1,0:T(8,128)(2,1)} %bitcast.16), calls=%async_computation.2 | async-start | bytes 1048576 | tf_op jit(solution)/shard_map/all_to_all | solution.py:60
  70.4 0.0 copy-done.5
  70.4 0.1 broadcast_compare_fusion.3
  70.4 8.8 %all-to-all-done.2 = bf16[8,2,8,16,128]{4,3,2,1,0:T(8,128)(2,1)S(1)} async-done(((bf16[8,2,8,16,128]{4,3,2,1,0:T(8,128)(2,1)}), bf16[8,2,8,16,128]{4,3,2,1,0:T(8,128)(2,1)S(1)}, u32[]{:S(2)}, u32[]{:S(2)}) %all-to-all-start.2) | async-done | bytes 524320 | tf_op jit(solution)/shard_map/all_to_all | solution.py:60
  79.2 0.0 copy-done.3
  79.2 0.4 fusion.7
  79.6 0.1 copy.61
  79.7 0.1 copy.62
  79.8 0.0 copy-start.4
  79.9 0.0 copy-start.6
  79.9 0.1 broadcast_in_dim.81
  79.9 12.8 %all_to_all.51 = bf16[8,256,128]{2,1,0:T(8,128)(2,1)S(1)} all-to-all(bf16[8,256,128]{2,1,0:T(8,128)(2,1)S(1)} %broadcast_in_dim.81), channel_id=1, replica_groups=mesh['hi'=16,'lo'=4,'rep'=8] {'rep'}, dimensions={0} | all-to-all | bytes 1048576 | tf_op jit(solution)/shard_map/all_to_all | solution.py:19
  92.8 0.1 reduce_sum.40
  92.8 0.0 copy-done
  92.8 0.0 copy-done.4
  92.9 0.0 copy-done.6
  92.9 0.9 convert_reduce_fusion.1
  93.7 0.2 fusion.21
  93.9 0.1 reshape.110
  94.0 23.5 %all_to_all.52 = f32[64,1,128]{2,1,0:T(1,128)S(1)} all-to-all(f32[64,1,128]{2,1,0:T(1,128)S(1)} %bitcast.81), channel_id=1, replica_groups=mesh['hi'=16,'lo'=4,'rep'=8] {'hi','lo'}, dimensions={0} | all-to-all | bytes 65536 | tf_op jit(solution)/shard_map/all_to_all | solution.py:12
  117.6 18.5 %all_to_all.53 = f32[64,1,128]{2,1,0:T(1,128)S(1)} all-to-all(f32[64,1,128]{2,1,0:T(1,128)S(1)} %broadcast_in_dim.82), channel_id=1, replica_groups=mesh['hi'=16,'lo'=4,'rep'=8] {'hi','lo'}, dimensions={0} | all-to-all | bytes 65536 | tf_op jit(solution)/shard_map/all_to_all | solution.py:19
  136.1 0.5 slice.27
  136.7 0.1 reshape.111
  136.8 0.7 copy.65
  (18 shorter events, 0.3 us)
Async XLA Ops:
  0.6 92.2 %copy-start = (bf16[128,32]{0,1:T(8,128)(2,1)S(1)}, bf16[128,32]{0,1:T(8,128)(2,1)}, u32[]{:S(2)}) copy-start(bf16[128,32]{0,1:T(8,128)(2,1)} %param.13) | copy-start | bytes 24580
  12.8 16.7 %copy-start.2 = (s32[2,8]{1,0:T(2,128)S(1)}, s32[2,8]{1,0:T(2,128)}, u32[]{:S(2)}) copy-start(s32[2,8]{1,0:T(2,128)} %param.10) | copy-start | bytes 196
  14.3 43.1 %all-to-all-start.1 = ((bf16[16,2,8704]{2,1,0:T(2,128)(2,1)}), bf16[16,2,8704]{2,1,0:T(2,128)(2,1)S(1)}, u32[]{:S(2)}, u32[]{:S(2)}) async-start(bf16[16,2,8704]{2,1,0:T(2,128)(2,1)} %reshape.137), calls=%async_computation.1 | async-start | bytes 1114112 | tf_op jit(solution)/shard_map/all_to_all | solution.py:42
  58.3 1.0 copy-start.1
  59.3 0.9 slice-start
  63.9 6.4 %copy-start.5 = (s32[2]{0:T(128)S(1)}, s32[2]{0:T(128)}, u32[]{:S(2)}) copy-start(s32[2]{0:T(128)} %param.11) | copy-start | bytes 28
  63.9 15.3 %copy-start.3 = (bf16[2,8,128,128]{3,2,1,0:T(8,128)(2,1)S(1)}, bf16[2,8,128,128]{3,2,1,0:T(8,128)(2,1)}, u32[]{:S(2)}) copy-start(bf16[2,8,128,128]{3,2,1,0:T(8,128)(2,1)} %param.12) | copy-start | bytes 1572868
  65.4 13.8 %all-to-all-start.2 = ((bf16[8,2,8,16,128]{4,3,2,1,0:T(8,128)(2,1)}), bf16[8,2,8,16,128]{4,3,2,1,0:T(8,128)(2,1)S(1)}, u32[]{:S(2)}, u32[]{:S(2)}) async-start(bf16[8,2,8,16,128]{4,3,2,1,0:T(8,128)(2,1)} %bitcast.16), calls=%async_computation.2 | async-start | bytes 1048576 | tf_op jit(solution)/shard_map/all_to_all | solution.py:60
  79.8 13.0 %copy-start.4 = (bf16[256,32]{0,1:T(8,128)(2,1)S(1)}, bf16[256,32]{0,1:T(8,128)(2,1)}, u32[]{:S(2)}) copy-start(bf16[256,32]{0,1:T(8,128)(2,1)} %param.15) | copy-start | bytes 49156
  79.9 13.0 %copy-start.6 = (f32[32]{0:T(128)S(1)}, f32[32]{0:T(128)}, u32[]{:S(2)}) copy-start(f32[32]{0:T(128)} %param.14) | copy-start | bytes 388

commit v4 on v2

--- a/solution.py
+++ b/solution.py
@@ -51,8 +51,10 @@
     pick = (pos[:, :, None] == target).astype(jnp.bfloat16)
     needed = jnp.einsum("fqg,qgn->qfn", values, pick, preferred_element_type=jnp.float32).astype(jnp.bfloat16)
 
-    peer_parts = part_of.reshape(rb, reps, slots_dev).transpose(1, 0, 2)
-    outgoing = needed[peer_parts]
+    peer_parts = part_of.reshape(rb, reps, slots_dev).transpose(1, 0, 2).reshape(-1)
+    choose = (peer_parts[:, None] == part_ids[None, :]).astype(jnp.bfloat16)
+    outgoing = jnp.dot(choose, needed.reshape(parts, -1), preferred_element_type=jnp.float32)
+    outgoing = outgoing.astype(jnp.bfloat16).reshape(reps, rb, slots_dev, cols_dev, size_blk)
     incoming = lax.all_to_all(outgoing, "rep", 0, 0, tiled=True)
 
     slot_ids = lax.axis_index("rep") * slots_dev + jnp.arange(slots_dev, dtype=jnp.int32)

time: 135 us -> 135 us (level)
    gather x1 -> x0, local copies, waits for them, and re-layouts: 1.48 us -> none  [on_device(): outgoing = needed[peer_parts]]
where the time goes in v4:
time: 135 us
  blocking collectives  60.3 us (45%)
  waiting for transfers between devices  33.8 us (25%)
  starting transfers between devices  23.5 us (17%)
  local copies, waits for them, and re-layouts  8.53 us (6%)
  matrix products  6.41 us (5%)
    all_to_all x2, blocking collectives, spread(): return lax.all_to_all(wide, axis_name, 0, 0, tiled=True)  31.3 us
    all_to_all x1, waiting for transfers between devices, on_device(): lax.all_to_all(wide, 'row', 0, 3, tiled=True)  25 us
    all_to_all x1, blocking collectives, sum_over(): got = lax.all_to_all(pieces, axis_name, 0, 0, tiled=True)  20.2 us
    all_to_all x1, starting transfers between devices, on_device(): lax.all_to_all(wide, 'row', 0, 3, tiled=True)  18.6 us
    all_to_all x1, waiting for transfers between devices, on_device(): incoming = lax.all_to_all(outgoing, 'rep', 0, 0, tiled=True)  8.81 us
    all_gather x1, blocking collectives, on_device(): cols_all = lax.all_gather(block_cols, 'rep', axis=1, tiled=True)  8.77 us
    all_to_all x1, starting transfers between devices, on_device(): incoming = lax.all_to_all(outgoing, 'rep', 0, 0, tiled=True)  4.91 us
    dot_general x1, matrix products, on_device(): jnp.einsum('fqg,qgn->qfn', values, pick, preferred_element_type=jnp.float32)  3.69 us
  transfers between devices with their start and end apart: 2, of which 2 were waited for; matrix products, arithmetic and copies ran while one was open for 0% of the time, Pallas kernels for 0%

profile of v4, /device:TPU:8, one launch (start us, length us, event | category | flops | bytes accessed | tf_op | source)
XLA Modules:
  0.0 134.7 jit_solution(16969461694364146127)
XLA Ops:
  0.6 0.0 copy-start
  0.6 0.7 fusion.21
  1.3 0.2 convert_reduce_fusion
  1.5 0.9 convolution_convert_fusion.1
  2.5 0.1 copy.55
  2.6 0.1 copy.56
  2.7 0.3 broadcast_bitcast_fusion
  3.0 0.0 copy-start.2
  3.0 1.6 %reshape.134 = bf16[64,2,2176]{2,1,0:T(2,128)(2,1)} reshape(bf16[64,17,4,64]{3,2,1,0:T(4,128)(2,1)S(1)} %broadcast_bitcast_fusion) | data formatting | bytes 1114112
  4.6 18.6 %all-to-all-start = ((bf16[64,2,2176]{2,1,0:T(2,128)(2,1)}), bf16[64,2,2176]{2,1,0:T(2,128)(2,1)S(1)}, u32[]{:S(2)}, u32[]{:S(2)}) async-start(bf16[64,2,2176]{2,1,0:T(2,128)(2,1)} %reshape.134), calls=%async_computation | async-start | bytes 1114112 | tf_op jit(solution)/shard_map/all_to_all | solution.py:39
  23.2 0.0 copy-done.2
  23.2 8.8 %all-gather = s32[8,8,2]{1,2,0:T(2,128)S(1)} all-gather(s32[1,8,2]{1,2,0:T(2,128)S(1)} %bitcast.80), channel_id=1, replica_groups=mesh['row'=64,'rep'=8] {'rep'}, dimensions={0}, use_global_device_ids=true | all-gather | bytes 576 | tf_op jit(solution)/shard_map/all_gather | solution.py:43
  32.0 0.1 reshape.124
  32.1 0.1 reshape.116
  32.2 0.1 eq.34
  32.3 0.1 select_reduce_fusion
  32.4 0.1 iota_add_fusion
  32.5 25.0 %all-to-all-done = bf16[64,2,2176]{2,1,0:T(2,128)(2,1)S(1)} async-done(((bf16[64,2,2176]{2,1,0:T(2,128)(2,1)}), bf16[64,2,2176]{2,1,0:T(2,128)(2,1)S(1)}, u32[]{:S(2)}, u32[]{:S(2)}) %all-to-all-start) | async-done | bytes 557088 | tf_op jit(solution)/shard_map/all_to_all | solution.py:39
  57.4 0.7 reshape.135
  58.1 0.4 bitcast_bitcast_fusion
  58.5 0.0 copy-start.1
  58.5 0.6 slice.22
  59.1 0.3 copy.57
  59.4 0.1 copy-done.1
  59.5 0.0 slice-start
  59.5 1.3 %copy.59 = bf16[16,64,256]{2,0,1:T(8,128)(2,1)S(1)} copy(bf16[16,64,256]{1,0,2:T(8,128)(2,1)S(1)} %bitcast.70) | data formatting | bytes 1048576 | tf_op jit(solution)/shard_map/slice | solution.py:41
  60.9 0.0 slice-done
  60.9 0.1 copy.58
  61.0 3.7 %fusion.4 = bf16[64,16,128]{2,1,0:T(8,128)(2,1)S(1)} fusion(bf16[16,64,256]{2,0,1:T(8,128)(2,1)S(1)} %copy.59, s32[64,128]{1,0:T(8,128)S(1)} %iota_add_fusion, s32[64,256]{1,0:T(8,128)S(1)} %copy.58), kind=kOutput, calls=%fused_computation.5 | convolution fusion | flops 69337088 | bytes 884736 | tf_op jit(solution)/shard_map/fqg,qgn->qfn/dot_general | solution.py:52
  64.7 0.3 convolution_convert_fusion
  65.0 0.0 copy-start.5
  65.1 0.0 copy-start.3
  65.1 0.9 copy.60
  66.0 4.9 %all-to-all-start.1 = ((bf16[8,2,8,16,128]{4,3,2,1,0:T(8,128)(2,1)}), bf16[8,2,8,16,128]{4,3,2,1,0:T(8,128)(2,1)S(1)}, u32[]{:S(2)}, u32[]{:S(2)}) async-start(bf16[8,2,8,16,128]{4,3,2,1,0:T(8,128)(2,1)} %copy.60), calls=%async_computation.1 | async-start | bytes 1048576 | tf_op jit(solution)/shard_map/all_to_all | solution.py:58
  70.9 0.0 copy-done.5
  70.9 0.1 broadcast_compare_fusion.3
  71.0 8.8 %all-to-all-done.1 = bf16[8,2,8,16,128]{4,3,2,1,0:T(8,128)(2,1)S(1)} async-done(((bf16[8,2,8,16,128]{4,3,2,1,0:T(8,128)(2,1)}), bf16[8,2,8,16,128]{4,3,2,1,0:T(8,128)(2,1)S(1)}, u32[]{:S(2)}, u32[]{:S(2)}) %all-to-all-start.1) | async-done | bytes 524320 | tf_op jit(solution)/shard_map/all_to_all | solution.py:58
  79.8 0.0 copy-done.3
  79.8 0.4 fusion.7
  80.2 0.1 copy.62
  80.2 0.1 copy.63
  80.4 0.0 copy-start.4
  80.4 0.0 copy-start.6
  80.4 0.1 broadcast_in_dim.39
  80.5 12.8 %all_to_all.35 = bf16[8,256,128]{2,1,0:T(8,128)(2,1)S(1)} all-to-all(bf16[8,256,128]{2,1,0:T(8,128)(2,1)S(1)} %broadcast_in_dim.39), channel_id=1, replica_groups=mesh['row'=64,'rep'=8] {'rep'}, dimensions={0} | all-to-all | bytes 1048576 | tf_op jit(solution)/shard_map/all_to_all | solution.py:17
  93.3 0.1 reduce_sum.40
  93.4 0.0 copy-done
  93.4 0.0 copy-done.4
  93.4 0.0 copy-done.6
  93.4 0.9 convert_reduce_fusion.1
  94.3 0.2 fusion.24
  94.5 0.1 reshape.119
  94.6 20.2 %all_to_all.36 = f32[64,1,128]{2,1,0:T(1,128)S(1)} all-to-all(f32[64,1,128]{2,1,0:T(1,128)S(1)} %bitcast.76), channel_id=1, replica_groups=mesh['row'=64,'rep'=8] {'row'}, dimensions={0} | all-to-all | bytes 65536 | tf_op jit(solution)/shard_map/all_to_all | solution.py:10
  114.8 18.5 %all_to_all.37 = f32[64,1,128]{2,1,0:T(1,128)S(1)} all-to-all(f32[64,1,128]{2,1,0:T(1,128)S(1)} %broadcast_in_dim.40), channel_id=1, replica_groups=mesh['row'=64,'rep'=8] {'row'}, dimensions={0} | all-to-all | bytes 65536 | tf_op jit(solution)/shard_map/all_to_all | solution.py:17
  133.4 0.5 slice.25
  133.9 0.1 reshape.120
  134.0 0.7 copy.66
  (13 shorter events, 0.2 us)
Async XLA Ops:
  0.6 92.7 %copy-start = (bf16[128,32]{0,1:T(8,128)(2,1)S(1)}, bf16[128,32]{0,1:T(8,128)(2,1)}, u32[]{:S(2)}) copy-start(bf16[128,32]{0,1:T(8,128)(2,1)} %param.13) | copy-start | bytes 24580
  3.0 20.2 %copy-start.2 = (s32[2,8]{1,0:T(2,128)S(1)}, s32[2,8]{1,0:T(2,128)}, u32[]{:S(2)}) copy-start(s32[2,8]{1,0:T(2,128)} %param.10) | copy-start | bytes 196
  4.6 52.8 %all-to-all-start = ((bf16[64,2,2176]{2,1,0:T(2,128)(2,1)}), bf16[64,2,2176]{2,1,0:T(2,128)(2,1)S(1)}, u32[]{:S(2)}, u32[]{:S(2)}) async-start(bf16[64,2,2176]{2,1,0:T(2,128)(2,1)} %reshape.134), calls=%async_computation | async-start | bytes 1114112 | tf_op jit(solution)/shard_map/all_to_all | solution.py:39
  58.5 1.0 copy-start.1
  59.5 1.4 %slice-start = ((bf16[1,17,64,64,4]{2,4,1,3,0:T(4,128)(2,1)}), bf16[1,1,64,64,4]{2,4,1,3,0:T(4,128)(2,1)S(1)}, s32[]{:S(2)}) async-start(bf16[1,17,64,64,4]{2,4,1,3,0:T(4,128)(2,1)} %copy-done.1), calls=%async_computation.5 | async-start | bytes 131072 | tf_op jit(solution)/shard_map/slice | solution.py:40
  65.0 5.8 %copy-start.5 = (s32[2]{0:T(128)S(1)}, s32[2]{0:T(128)}, u32[]{:S(2)}) copy-start(s32[2]{0:T(128)} %param.11) | copy-start | bytes 28
  65.1 14.7 %copy-start.3 = (bf16[2,8,128,128]{3,2,1,0:T(8,128)(2,1)S(1)}, bf16[2,8,128,128]{3,2,1,0:T(8,128)(2,1)}, u32[]{:S(2)}) copy-start(bf16[2,8,128,128]{3,2,1,0:T(8,128)(2,1)} %param.12) | copy-start | bytes 1572868
  66.0 13.8 %all-to-all-start.1 = ((bf16[8,2,8,16,128]{4,3,2,1,0:T(8,128)(2,1)}), bf16[8,2,8,16,128]{4,3,2,1,0:T(8,128)(2,1)S(1)}, u32[]{:S(2)}, u32[]{:S(2)}) async-start(bf16[8,2,8,16,128]{4,3,2,1,0:T(8,128)(2,1)} %copy.60), calls=%async_computation.1 | async-start | bytes 1048576 | tf_op jit(solution)/shard_map/all_to_all | solution.py:58
  80.4 13.0 %copy-start.4 = (bf16[256,32]{0,1:T(8,128)(2,1)S(1)}, bf16[256,32]{0,1:T(8,128)(2,1)}, u32[]{:S(2)}) copy-start(bf16[256,32]{0,1:T(8,128)(2,1)} %param.15) | copy-start | bytes 49156
  80.4 13.0 %copy-start.6 = (f32[32]{0:T(128)S(1)}, f32[32]{0:T(128)}, u32[]{:S(2)}) copy-start(f32[32]{0:T(128)} %param.14) | copy-start | bytes 388

commit v5 on v4

--- a/solution.py
+++ b/solution.py
@@ -28,16 +28,16 @@
     same = destination[:, None] == destination[None, :]
     before = jnp.arange(rows_part)[:, None] > jnp.arange(rows_part)[None, :]
     rank = jnp.sum(same & before, axis=1)
-    slot = destination * per_pair + rank
+    slot = rank * parts + destination
     place = (slot[:, None] == jnp.arange(rows_part)[None, :]).astype(jnp.bfloat16)
     pos_row = (owner_index % rows_part).astype(jnp.bfloat16)
     loader = jnp.concatenate([features.T, pos_row[None, :]], axis=0)
     packet = jnp.dot(loader, place, preferred_element_type=jnp.float32).astype(jnp.bfloat16)
     width = cols_dev + 1
-    packet = packet.reshape(width, parts, per_pair)
+    packet = packet.reshape(width, per_pair, parts)
     wide = jnp.broadcast_to(packet[None], (parts,) + packet.shape)
-    grouped = lax.all_to_all(wide, "row", 0, 3, tiled=True).reshape(width, parts, rows_part)
-    pos = grouped[cols_dev].astype(jnp.int32)
+    grouped = lax.all_to_all(wide, "row", 0, 2, tiled=True)[0]
+    pos = grouped[cols_dev].T.astype(jnp.int32)
     values = grouped[:cols_dev]
 
     cols_all = lax.all_gather(block_cols, "rep", axis=1, tiled=True)
@@ -49,7 +49,7 @@
     node_ids = jnp.arange(size_blk, dtype=jnp.int32)
     target = half[:, None, None] * size_blk + node_ids[None, None, :]
     pick = (pos[:, :, None] == target).astype(jnp.bfloat16)
-    needed = jnp.einsum("fqg,qgn->qfn", values, pick, preferred_element_type=jnp.float32).astype(jnp.bfloat16)
+    needed = jnp.einsum("fgq,qgn->qfn", values, pick, preferred_element_type=jnp.float32).astype(jnp.bfloat16)
 
     peer_parts = part_of.reshape(rb, reps, slots_dev).transpose(1, 0, 2).reshape(-1)
     choose = (peer_parts[:, None] == part_ids[None, :]).astype(jnp.bfloat16)

time: 135 us -> 134 us (level)
    unnamed x20 -> x17, local copies, waits for them, and re-layouts: 3.54 us -> 3.11 us
where the time goes in v5:
time: 134 us
  blocking collectives  60.3 us (45%)
  waiting for transfers between devices  33.8 us (25%)
  starting transfers between devices  23.5 us (18%)
  local copies, waits for them, and re-layouts  7.86 us (6%)
  matrix products  6.41 us (5%)
    all_to_all x2, blocking collectives, spread(): return lax.all_to_all(wide, axis_name, 0, 0, tiled=True)  31.3 us
    all_to_all x1, waiting for transfers between devices, on_device(): grouped = lax.all_to_all(wide, 'row', 0, 2, tiled=True)[0]  25 us
    all_to_all x1, blocking collectives, sum_over(): got = lax.all_to_all(pieces, axis_name, 0, 0, tiled=True)  20.2 us
    all_to_all x1, starting transfers between devices, on_device(): grouped = lax.all_to_all(wide, 'row', 0, 2, tiled=True)[0]  18.6 us
    all_to_all x1, waiting for transfers between devices, on_device(): incoming = lax.all_to_all(outgoing, 'rep', 0, 0, tiled=True)  8.81 us
    all_gather x1, blocking collectives, on_device(): cols_all = lax.all_gather(block_cols, 'rep', axis=1, tiled=True)  8.77 us
    all_to_all x1, starting transfers between devices, on_device(): incoming = lax.all_to_all(outgoing, 'rep', 0, 0, tiled=True)  4.92 us
    dot_general x1, matrix products, on_device(): jnp.einsum('fgq,qgn->qfn', values, pick, preferred_element_type=jnp.float32)  3.69 us
  transfers between devices with their start and end apart: 2, of which 2 were waited for; matrix products, arithmetic and copies ran while one was open for 0% of the time, Pallas kernels for 0%

profile of v5, /device:TPU:8, one launch (start us, length us, event | category | flops | bytes accessed | tf_op | source)
XLA Modules:
  0.0 134.0 jit_solution(5419342844802911727)
XLA Ops:
  0.6 0.0 copy-start
  0.6 0.7 fusion.21
  1.3 0.2 convert_reduce_fusion
  1.5 0.9 convolution_convert_fusion.1
  2.5 0.1 broadcast_in_dim.35
  2.6 0.3 broadcast_in_dim.36
  2.9 0.0 copy-start.1
  2.9 1.6 %reshape.129 = bf16[64,2,2176]{2,1,0:T(2,128)(2,1)} reshape(bf16[64,17,4,64]{3,2,1,0:T(4,128)(2,1)S(1)} %broadcast_in_dim.36) | data formatting | bytes 1114112
  4.5 18.6 %all-to-all-start = ((bf16[64,2,2176]{2,1,0:T(2,128)(2,1)}), bf16[64,2,2176]{2,1,0:T(2,128)(2,1)S(1)}, u32[]{:S(2)}, u32[]{:S(2)}) async-start(bf16[64,2,2176]{2,1,0:T(2,128)(2,1)} %reshape.129), calls=%async_computation | async-start | bytes 1114112 | tf_op jit(solution)/shard_map/all_to_all | solution.py:39
  23.0 0.0 copy-done.1
  23.0 8.8 %all-gather = s32[8,8,2]{1,2,0:T(2,128)S(1)} all-gather(s32[1,8,2]{1,2,0:T(2,128)S(1)} %bitcast.77), channel_id=1, replica_groups=mesh['row'=64,'rep'=8] {'rep'}, dimensions={0}, use_global_device_ids=true | all-gather | bytes 576 | tf_op jit(solution)/shard_map/all_gather | solution.py:43
  31.8 0.1 reshape.119
  31.9 0.1 reshape.111
  32.0 0.1 eq.34
  32.1 0.1 select_reduce_fusion
  32.2 0.1 iota_add_fusion
  32.3 25.0 %all-to-all-done = bf16[64,2,2176]{2,1,0:T(2,128)(2,1)S(1)} async-done(((bf16[64,2,2176]{2,1,0:T(2,128)(2,1)}), bf16[64,2,2176]{2,1,0:T(2,128)(2,1)S(1)}, u32[]{:S(2)}, u32[]{:S(2)}) %all-to-all-start) | async-done | bytes 557088 | tf_op jit(solution)/shard_map/all_to_all | solution.py:39
  57.3 0.7 reshape.130
  58.0 0.6 slice.22
  58.6 0.3 copy.49
  58.8 1.4 %copy.51 = bf16[16,256,64]{1,0,2:T(8,128)(2,1)S(1)} copy(bf16[16,256,64]{2,0,1:T(8,128)(2,1)S(1)} %bitcast.67) | data formatting | bytes 1048576 | tf_op jit(solution)/shard_map/slice | solution.py:41
  60.2 0.1 copy.50
  60.3 3.7 %fusion.4 = bf16[64,16,128]{2,1,0:T(8,128)(2,1)S(1)} fusion(bf16[16,256,64]{1,0,2:T(8,128)(2,1)S(1)} %copy.51, s32[64,128]{1,0:T(8,128)S(1)} %iota_add_fusion, s32[64,256]{1,0:T(8,128)S(1)} %copy.50), kind=kOutput, calls=%fused_computation.5 | convolution fusion | flops 69337088 | bytes 884736 | tf_op jit(solution)/shard_map/fgq,qgn->qfn/dot_general | solution.py:52
  64.0 0.3 convolution_convert_fusion
  64.4 0.0 copy-start.4
  64.4 0.0 copy-start.2
  64.4 0.9 copy.52
  65.3 4.9 %all-to-all-start.1 = ((bf16[8,2,8,16,128]{4,3,2,1,0:T(8,128)(2,1)}), bf16[8,2,8,16,128]{4,3,2,1,0:T(8,128)(2,1)S(1)}, u32[]{:S(2)}, u32[]{:S(2)}) async-start(bf16[8,2,8,16,128]{4,3,2,1,0:T(8,128)(2,1)} %copy.52), calls=%async_computation.1 | async-start | bytes 1048576 | tf_op jit(solution)/shard_map/all_to_all | solution.py:58
  70.2 0.0 copy-done.4
  70.2 0.1 broadcast_compare_fusion.3
  70.3 8.8 %all-to-all-done.1 = bf16[8,2,8,16,128]{4,3,2,1,0:T(8,128)(2,1)S(1)} async-done(((bf16[8,2,8,16,128]{4,3,2,1,0:T(8,128)(2,1)}), bf16[8,2,8,16,128]{4,3,2,1,0:T(8,128)(2,1)S(1)}, u32[]{:S(2)}, u32[]{:S(2)}) %all-to-all-start.1) | async-done | bytes 524320 | tf_op jit(solution)/shard_map/all_to_all | solution.py:58
  79.1 0.0 copy-done.2
  79.1 0.4 fusion.7
  79.5 0.1 copy.54
  79.6 0.1 copy.55
  79.7 0.0 copy-start.3
  79.7 0.0 copy-start.5
  79.7 0.1 broadcast_in_dim.39
  79.8 12.8 %all_to_all.35 = bf16[8,256,128]{2,1,0:T(8,128)(2,1)S(1)} all-to-all(bf16[8,256,128]{2,1,0:T(8,128)(2,1)S(1)} %broadcast_in_dim.39), channel_id=1, replica_groups=mesh['row'=64,'rep'=8] {'rep'}, dimensions={0} | all-to-all | bytes 1048576 | tf_op jit(solution)/shard_map/all_to_all | solution.py:17
  92.6 0.1 reduce_sum.40
  92.7 0.0 copy-done
  92.7 0.0 copy-done.3
  92.7 0.0 copy-done.5
  92.7 0.9 convert_reduce_fusion.1
  93.6 0.2 fusion.24
  93.8 0.1 reshape.114
  93.9 20.2 %all_to_all.36 = f32[64,1,128]{2,1,0:T(1,128)S(1)} all-to-all(f32[64,1,128]{2,1,0:T(1,128)S(1)} %bitcast.73), channel_id=1, replica_groups=mesh['row'=64,'rep'=8] {'row'}, dimensions={0} | all-to-all | bytes 65536 | tf_op jit(solution)/shard_map/all_to_all | solution.py:10
  114.2 18.5 %all_to_all.37 = f32[64,1,128]{2,1,0:T(1,128)S(1)} all-to-all(f32[64,1,128]{2,1,0:T(1,128)S(1)} %broadcast_in_dim.40), channel_id=1, replica_groups=mesh['row'=64,'rep'=8] {'row'}, dimensions={0} | all-to-all | bytes 65536 | tf_op jit(solution)/shard_map/all_to_all | solution.py:17
  132.7 0.5 slice.25
  133.2 0.1 reshape.115
  133.3 0.7 copy.58
  (14 shorter events, 0.2 us)
Async XLA Ops:
  0.6 92.0 %copy-start = (bf16[128,32]{0,1:T(8,128)(2,1)S(1)}, bf16[128,32]{0,1:T(8,128)(2,1)}, u32[]{:S(2)}) copy-start(bf16[128,32]{0,1:T(8,128)(2,1)} %param.13) | copy-start | bytes 24580
  2.9 20.2 %copy-start.1 = (s32[2,8]{1,0:T(2,128)S(1)}, s32[2,8]{1,0:T(2,128)}, u32[]{:S(2)}) copy-start(s32[2,8]{1,0:T(2,128)} %param.10) | copy-start | bytes 196
  4.5 52.8 %all-to-all-start = ((bf16[64,2,2176]{2,1,0:T(2,128)(2,1)}), bf16[64,2,2176]{2,1,0:T(2,128)(2,1)S(1)}, u32[]{:S(2)}, u32[]{:S(2)}) async-start(bf16[64,2,2176]{2,1,0:T(2,128)(2,1)} %reshape.129), calls=%async_computation | async-start | bytes 1114112 | tf_op jit(solution)/shard_map/all_to_all | solution.py:39
  64.4 5.8 %copy-start.4 = (s32[2]{0:T(128)S(1)}, s32[2]{0:T(128)}, u32[]{:S(2)}) copy-start(s32[2]{0:T(128)} %param.11) | copy-start | bytes 28
  64.4 14.7 %copy-start.2 = (bf16[2,8,128,128]{3,2,1,0:T(8,128)(2,1)S(1)}, bf16[2,8,128,128]{3,2,1,0:T(8,128)(2,1)}, u32[]{:S(2)}) copy-start(bf16[2,8,128,128]{3,2,1,0:T(8,128)(2,1)} %param.12) | copy-start | bytes 1572868
  65.3 13.8 %all-to-all-start.1 = ((bf16[8,2,8,16,128]{4,3,2,1,0:T(8,128)(2,1)}), bf16[8,2,8,16,128]{4,3,2,1,0:T(8,128)(2,1)S(1)}, u32[]{:S(2)}, u32[]{:S(2)}) async-start(bf16[8,2,8,16,128]{4,3,2,1,0:T(8,128)(2,1)} %copy.52), calls=%async_computation.1 | async-start | bytes 1048576 | tf_op jit(solution)/shard_map/all_to_all | solution.py:58
  79.7 13.0 %copy-start.3 = (bf16[256,32]{0,1:T(8,128)(2,1)S(1)}, bf16[256,32]{0,1:T(8,128)(2,1)}, u32[]{:S(2)}) copy-start(bf16[256,32]{0,1:T(8,128)(2,1)} %param.15) | copy-start | bytes 49156
  79.7 13.0 %copy-start.5 = (f32[32]{0:T(128)S(1)}, f32[32]{0:T(128)}, u32[]{:S(2)}) copy-start(f32[32]{0:T(128)} %param.14) | copy-start | bytes 388

commit v6 on v5

--- a/solution.py
+++ b/solution.py
@@ -49,7 +49,8 @@
     node_ids = jnp.arange(size_blk, dtype=jnp.int32)
     target = half[:, None, None] * size_blk + node_ids[None, None, :]
     pick = (pos[:, :, None] == target).astype(jnp.bfloat16)
-    needed = jnp.einsum("fgq,qgn->qfn", values, pick, preferred_element_type=jnp.float32).astype(jnp.bfloat16)
+    needed = jnp.einsum("fgq,qgn->qfn", grouped, pick, preferred_element_type=jnp.float32).astype(jnp.bfloat16)
+    needed = needed[:, :cols_dev, :]
 
     peer_parts = part_of.reshape(rb, reps, slots_dev).transpose(1, 0, 2).reshape(-1)
     choose = (peer_parts[:, None] == part_ids[None, :]).astype(jnp.bfloat16)

time: 134 us -> 134 us (level)
    slice x3 -> x1, local copies, waits for them, and re-layouts: 2.19 us -> 0.02 us  [on_device(): needed = needed[:, :cols_dev, :]]
where the time goes in v6:
time: 134 us; the launch traced here: 133 us
  blocking collectives  60.3 us (45%)
  waiting for transfers between devices  33.8 us (25%)
  starting transfers between devices  23.5 us (18%)
  local copies, waits for them, and re-layouts  7.06 us (5%)
  matrix products  6.45 us (5%)
    all_to_all x2, blocking collectives, spread(): return lax.all_to_all(wide, axis_name, 0, 0, tiled=True)  31.3 us
    all_to_all x1, waiting for transfers between devices, on_device(): grouped = lax.all_to_all(wide, 'row', 0, 2, tiled=True)[0]  25 us
    all_to_all x1, blocking collectives, sum_over(): got = lax.all_to_all(pieces, axis_name, 0, 0, tiled=True)  20.2 us
    all_to_all x1, starting transfers between devices, on_device(): grouped = lax.all_to_all(wide, 'row', 0, 2, tiled=True)[0]  18.6 us
    all_to_all x1, waiting for transfers between devices, on_device(): incoming = lax.all_to_all(outgoing, 'rep', 0, 0, tiled=True)  8.81 us
    all_gather x1, blocking collectives, on_device(): cols_all = lax.all_gather(block_cols, 'rep', axis=1, tiled=True)  8.77 us
    all_to_all x1, starting transfers between devices, on_device(): incoming = lax.all_to_all(outgoing, 'rep', 0, 0, tiled=True)  4.92 us
    dot_general x1, matrix products, on_device(): jnp.einsum('fgq,qgn->qfn', grouped, pick, preferred_element_type=jnp.floa...  3.74 us
  transfers between devices with their start and end apart: 2, of which 2 were waited for; matrix products, arithmetic and copies ran while one was open for 0% of the time, Pallas kernels for 0%

profile of v6, /device:TPU:8, one launch (start us, length us, event | category | flops | bytes accessed | tf_op | source)
XLA Modules:
  0.0 133.2 jit_solution(12137546198798119520)
XLA Ops:
  0.6 0.0 copy-start
  0.6 0.7 fusion.18
  1.3 0.2 convert_reduce_fusion
  1.5 0.9 convolution_convert_fusion.1
  2.5 0.1 broadcast_in_dim.35
  2.6 0.3 broadcast_in_dim.36
  2.9 0.0 copy-start.1
  2.9 1.6 %reshape.128 = bf16[64,2,2176]{2,1,0:T(2,128)(2,1)} reshape(bf16[64,17,4,64]{3,2,1,0:T(4,128)(2,1)S(1)} %broadcast_in_dim.36) | data formatting | bytes 1114112
  4.5 18.6 %all-to-all-start = ((bf16[64,2,2176]{2,1,0:T(2,128)(2,1)}), bf16[64,2,2176]{2,1,0:T(2,128)(2,1)S(1)}, u32[]{:S(2)}, u32[]{:S(2)}) async-start(bf16[64,2,2176]{2,1,0:T(2,128)(2,1)} %reshape.128), calls=%async_computation | async-start | bytes 1114112 | tf_op jit(solution)/shard_map/all_to_all | solution.py:39
  23.0 0.0 copy-done.1
  23.0 8.8 %all-gather = s32[8,8,2]{1,2,0:T(2,128)S(1)} all-gather(s32[1,8,2]{1,2,0:T(2,128)S(1)} %bitcast.77), channel_id=1, replica_groups=mesh['row'=64,'rep'=8] {'rep'}, dimensions={0}, use_global_device_ids=true | all-gather | bytes 576 | tf_op jit(solution)/shard_map/all_gather | solution.py:43
  31.8 0.1 reshape.118
  31.9 0.1 reshape.110
  32.0 0.1 eq.34
  32.1 0.1 select_reduce_fusion
  32.2 0.1 iota_add_fusion
  32.3 25.0 %all-to-all-done = bf16[64,2,2176]{2,1,0:T(2,128)(2,1)S(1)} async-done(((bf16[64,2,2176]{2,1,0:T(2,128)(2,1)}), bf16[64,2,2176]{2,1,0:T(2,128)(2,1)S(1)}, u32[]{:S(2)}, u32[]{:S(2)}) %all-to-all-start) | async-done | bytes 557088 | tf_op jit(solution)/shard_map/all_to_all | solution.py:39
  57.3 0.7 reshape.129
  58.0 0.5 copy.48
  58.5 0.8 copy.50
  59.4 0.1 copy.49
  59.5 3.7 %fusion = bf16[64,17,128]{2,1,0:T(8,128)(2,1)S(1)} fusion(bf16[17,256,64]{1,0,2:T(8,128)(2,1)S(1)} %copy.50, s32[64,128]{1,0:T(8,128)S(1)} %iota_add_fusion, s32[64,256]{1,0:T(8,128)S(1)} %copy.49), kind=kOutput, calls=%fused_computation | convolution fusion | flops 73400320 | bytes 933888 | tf_op jit(solution)/shard_map/fgq,qgn->qfn/dot_general | solution.py:52
  63.3 0.3 convolution_convert_fusion
  63.6 0.0 copy-start.4
  63.6 0.0 copy-start.2
  63.6 0.9 copy.51
  64.5 4.9 %all-to-all-start.1 = ((bf16[8,2,8,16,128]{4,3,2,1,0:T(8,128)(2,1)}), bf16[8,2,8,16,128]{4,3,2,1,0:T(8,128)(2,1)S(1)}, u32[]{:S(2)}, u32[]{:S(2)}) async-start(bf16[8,2,8,16,128]{4,3,2,1,0:T(8,128)(2,1)} %copy.51), calls=%async_computation.1 | async-start | bytes 1048576 | tf_op jit(solution)/shard_map/all_to_all | solution.py:59
  69.5 0.0 copy-done.4
  69.5 0.1 broadcast_compare_fusion.3
  69.5 8.8 %all-to-all-done.1 = bf16[8,2,8,16,128]{4,3,2,1,0:T(8,128)(2,1)S(1)} async-done(((bf16[8,2,8,16,128]{4,3,2,1,0:T(8,128)(2,1)}), bf16[8,2,8,16,128]{4,3,2,1,0:T(8,128)(2,1)S(1)}, u32[]{:S(2)}, u32[]{:S(2)}) %all-to-all-start.1) | async-done | bytes 524320 | tf_op jit(solution)/shard_map/all_to_all | solution.py:59
  78.3 0.0 copy-done.2
  78.3 0.4 fusion.4
  78.7 0.1 copy.53
  78.8 0.1 copy.54
  78.9 0.0 copy-start.3
  78.9 0.0 copy-start.5
  79.0 0.1 broadcast_in_dim.39
  79.0 12.8 %all_to_all.35 = bf16[8,256,128]{2,1,0:T(8,128)(2,1)S(1)} all-to-all(bf16[8,256,128]{2,1,0:T(8,128)(2,1)S(1)} %broadcast_in_dim.39), channel_id=1, replica_groups=mesh['row'=64,'rep'=8] {'rep'}, dimensions={0} | all-to-all | bytes 1048576 | tf_op jit(solution)/shard_map/all_to_all | solution.py:17
  91.8 0.1 reduce_sum.40
  91.9 0.0 copy-done
  91.9 0.0 copy-done.3
  91.9 0.0 copy-done.5
  92.0 0.9 convert_reduce_fusion.1
  92.8 0.2 fusion.21
  93.0 0.1 reshape.113
  93.1 20.2 %all_to_all.36 = f32[64,1,128]{2,1,0:T(1,128)S(1)} all-to-all(f32[64,1,128]{2,1,0:T(1,128)S(1)} %bitcast.73), channel_id=1, replica_groups=mesh['row'=64,'rep'=8] {'row'}, dimensions={0} | all-to-all | bytes 65536 | tf_op jit(solution)/shard_map/all_to_all | solution.py:10
  113.4 18.5 %all_to_all.37 = f32[64,1,128]{2,1,0:T(1,128)S(1)} all-to-all(f32[64,1,128]{2,1,0:T(1,128)S(1)} %broadcast_in_dim.40), channel_id=1, replica_groups=mesh['row'=64,'rep'=8] {'row'}, dimensions={0} | all-to-all | bytes 65536 | tf_op jit(solution)/shard_map/all_to_all | solution.py:17
  131.9 0.5 slice.21
  132.5 0.1 reshape.114
  132.6 0.7 copy.57
  (15 shorter events, 0.2 us)
Async XLA Ops:
  0.6 91.3 %copy-start = (bf16[128,32]{0,1:T(8,128)(2,1)S(1)}, bf16[128,32]{0,1:T(8,128)(2,1)}, u32[]{:S(2)}) copy-start(bf16[128,32]{0,1:T(8,128)(2,1)} %param.13) | copy-start | bytes 24580
  2.9 20.2 %copy-start.1 = (s32[2,8]{1,0:T(2,128)S(1)}, s32[2,8]{1,0:T(2,128)}, u32[]{:S(2)}) copy-start(s32[2,8]{1,0:T(2,128)} %param.10) | copy-start | bytes 196
  4.5 52.8 %all-to-all-start = ((bf16[64,2,2176]{2,1,0:T(2,128)(2,1)}), bf16[64,2,2176]{2,1,0:T(2,128)(2,1)S(1)}, u32[]{:S(2)}, u32[]{:S(2)}) async-start(bf16[64,2,2176]{2,1,0:T(2,128)(2,1)} %reshape.128), calls=%async_computation | async-start | bytes 1114112 | tf_op jit(solution)/shard_map/all_to_all | solution.py:39
  63.6 5.8 %copy-start.4 = (s32[2]{0:T(128)S(1)}, s32[2]{0:T(128)}, u32[]{:S(2)}) copy-start(s32[2]{0:T(128)} %param.11) | copy-start | bytes 28
  63.6 14.7 %copy-start.2 = (bf16[2,8,128,128]{3,2,1,0:T(8,128)(2,1)S(1)}, bf16[2,8,128,128]{3,2,1,0:T(8,128)(2,1)}, u32[]{:S(2)}) copy-start(bf16[2,8,128,128]{3,2,1,0:T(8,128)(2,1)} %param.12) | copy-start | bytes 1572868
  64.5 13.8 %all-to-all-start.1 = ((bf16[8,2,8,16,128]{4,3,2,1,0:T(8,128)(2,1)}), bf16[8,2,8,16,128]{4,3,2,1,0:T(8,128)(2,1)S(1)}, u32[]{:S(2)}, u32[]{:S(2)}) async-start(bf16[8,2,8,16,128]{4,3,2,1,0:T(8,128)(2,1)} %copy.51), calls=%async_computation.1 | async-start | bytes 1048576 | tf_op jit(solution)/shard_map/all_to_all | solution.py:59
  78.9 13.0 %copy-start.3 = (bf16[256,32]{0,1:T(8,128)(2,1)S(1)}, bf16[256,32]{0,1:T(8,128)(2,1)}, u32[]{:S(2)}) copy-start(bf16[256,32]{0,1:T(8,128)(2,1)} %param.15) | copy-start | bytes 49156
  78.9 13.0 %copy-start.5 = (f32[32]{0:T(128)S(1)}, f32[32]{0:T(128)}, u32[]{:S(2)}) copy-start(f32[32]{0:T(128)} %param.14) | copy-start | bytes 388

commit v7 on v6

--- a/solution.py
+++ b/solution.py
@@ -74,14 +74,14 @@
     weight_term = jnp.dot(agg.T, dpre, preferred_element_type=jnp.float32)
     bias_term = jnp.sum(dpre.astype(jnp.float32), axis=0)
 
-    flat = jnp.concatenate([weight_term.reshape(-1), bias_term])
-    lanes = 128
-    chunk = lanes * (-(-flat.shape[0] // (parts * lanes)))
-    flat = jnp.pad(flat, (0, parts * chunk - flat.shape[0])).reshape(parts, chunk)
-    total = spread(sum_over(flat, "row", parts), "row", parts).reshape(-1)
-    n_w = weight_term.size
-    weight_grad = total[:n_w].reshape(weight_term.shape)
-    bias_grad = total[n_w:n_w + bias_term.shape[0]]
+    n_in, n_out = weight_term.shape
+    bias_row = jnp.pad(bias_term, (0, n_in - n_out))[None, :]
+    stacked = jnp.concatenate([weight_term.T, bias_row], axis=0)
+    per = -(-stacked.shape[0] // parts)
+    stacked = jnp.pad(stacked, ((0, parts * per - stacked.shape[0]), (0, 0)))
+    total = spread(sum_over(stacked, "row", parts), "row", parts).reshape(parts * per, n_in)
+    weight_grad = total[:n_out].T
+    bias_grad = total[n_out, :n_out]
     return (hidden, weight_grad, bias_grad)
 
 

time: 134 us -> 133 us (level)
    unnamed x17 -> x16, local copies, waits for them, and re-layouts: 3.11 us -> 2.42 us
where the time goes in v7:
time: 133 us
  blocking collectives  60.3 us (45%)
  waiting for transfers between devices  33.8 us (25%)
  starting transfers between devices  23.5 us (18%)
  local copies, waits for them, and re-layouts  6.78 us (5%)
  matrix products  6.39 us (5%)
  other arithmetic  1.35 us (1%)
    all_to_all x2, blocking collectives, spread(): return lax.all_to_all(wide, axis_name, 0, 0, tiled=True)  31.3 us
    all_to_all x1, waiting for transfers between devices, on_device(): grouped = lax.all_to_all(wide, 'row', 0, 2, tiled=True)[0]  25 us
    all_to_all x1, blocking collectives, sum_over(): got = lax.all_to_all(pieces, axis_name, 0, 0, tiled=True)  20.2 us
    all_to_all x1, starting transfers between devices, on_device(): grouped = lax.all_to_all(wide, 'row', 0, 2, tiled=True)[0]  18.6 us
    all_to_all x1, waiting for transfers between devices, on_device(): incoming = lax.all_to_all(outgoing, 'rep', 0, 0, tiled=True)  8.81 us
    all_gather x1, blocking collectives, on_device(): cols_all = lax.all_gather(block_cols, 'rep', axis=1, tiled=True)  8.77 us
    all_to_all x1, starting transfers between devices, on_device(): incoming = lax.all_to_all(outgoing, 'rep', 0, 0, tiled=True)  4.92 us
    dot_general x1, matrix products, on_device(): jnp.einsum('fgq,qgn->qfn', grouped, pick, preferred_element_type=jnp.floa...  3.74 us
  transfers between devices with their start and end apart: 2, of which 2 were waited for; matrix products, arithmetic and copies ran while one was open for 0% of the time, Pallas kernels for 0%

profile of v7, /device:TPU:8, one launch (start us, length us, event | category | flops | bytes accessed | tf_op | source)
XLA Modules:
  0.0 133.0 jit_solution(4461811390317609364)
XLA Ops:
  0.6 0.0 copy-start
  0.6 0.7 fusion.18
  1.3 0.2 convert_reduce_fusion
  1.5 0.9 convolution_convert_fusion.1
  2.5 0.1 broadcast_in_dim.37
  2.6 0.3 broadcast_in_dim.38
  2.9 0.0 copy-start.1
  2.9 1.6 %reshape.116 = bf16[64,2,2176]{2,1,0:T(2,128)(2,1)} reshape(bf16[64,17,4,64]{3,2,1,0:T(4,128)(2,1)S(1)} %broadcast_in_dim.38) | data formatting | bytes 1114112
  4.5 18.6 %all-to-all-start = ((bf16[64,2,2176]{2,1,0:T(2,128)(2,1)}), bf16[64,2,2176]{2,1,0:T(2,128)(2,1)S(1)}, u32[]{:S(2)}, u32[]{:S(2)}) async-start(bf16[64,2,2176]{2,1,0:T(2,128)(2,1)} %reshape.116), calls=%async_computation | async-start | bytes 1114112 | tf_op jit(solution)/shard_map/all_to_all | solution.py:39
  23.0 0.0 copy-done.1
  23.0 8.8 %all-gather = s32[8,8,2]{1,2,0:T(2,128)S(1)} all-gather(s32[1,8,2]{1,2,0:T(2,128)S(1)} %bitcast.85), channel_id=1, replica_groups=mesh['row'=64,'rep'=8] {'rep'}, dimensions={0}, use_global_device_ids=true | all-gather | bytes 576 | tf_op jit(solution)/shard_map/all_gather | solution.py:43
  31.8 0.1 reshape.113
  31.9 0.1 reshape.106
  32.0 0.1 eq.34
  32.1 0.1 select_reduce_fusion
  32.2 0.1 iota_add_fusion
  32.3 25.0 %all-to-all-done = bf16[64,2,2176]{2,1,0:T(2,128)(2,1)S(1)} async-done(((bf16[64,2,2176]{2,1,0:T(2,128)(2,1)}), bf16[64,2,2176]{2,1,0:T(2,128)(2,1)S(1)}, u32[]{:S(2)}, u32[]{:S(2)}) %all-to-all-start) | async-done | bytes 557088 | tf_op jit(solution)/shard_map/all_to_all | solution.py:39
  57.3 0.7 reshape.117
  58.0 0.5 copy.34
  58.5 0.8 copy.36
  59.4 0.1 copy.35
  59.5 3.7 %fusion = bf16[64,17,128]{2,1,0:T(8,128)(2,1)S(1)} fusion(bf16[17,256,64]{1,0,2:T(8,128)(2,1)S(1)} %copy.36, s32[64,128]{1,0:T(8,128)S(1)} %iota_add_fusion, s32[64,256]{1,0:T(8,128)S(1)} %copy.35), kind=kOutput, calls=%fused_computation | convolution fusion | flops 73400320 | bytes 933888 | tf_op jit(solution)/shard_map/fgq,qgn->qfn/dot_general | solution.py:52
  63.3 0.3 convolution_convert_fusion
  63.6 0.0 copy-start.4
  63.6 0.0 copy-start.2
  63.6 0.9 copy.37
  64.5 4.9 %all-to-all-start.1 = ((bf16[8,2,8,16,128]{4,3,2,1,0:T(8,128)(2,1)}), bf16[8,2,8,16,128]{4,3,2,1,0:T(8,128)(2,1)S(1)}, u32[]{:S(2)}, u32[]{:S(2)}) async-start(bf16[8,2,8,16,128]{4,3,2,1,0:T(8,128)(2,1)} %copy.37), calls=%async_computation.1 | async-start | bytes 1048576 | tf_op jit(solution)/shard_map/all_to_all | solution.py:59
  69.5 0.0 copy-done.4
  69.5 0.1 broadcast_compare_fusion.3
  69.5 8.8 %all-to-all-done.1 = bf16[8,2,8,16,128]{4,3,2,1,0:T(8,128)(2,1)S(1)} async-done(((bf16[8,2,8,16,128]{4,3,2,1,0:T(8,128)(2,1)}), bf16[8,2,8,16,128]{4,3,2,1,0:T(8,128)(2,1)S(1)}, u32[]{:S(2)}, u32[]{:S(2)}) %all-to-all-start.1) | async-done | bytes 524320 | tf_op jit(solution)/shard_map/all_to_all | solution.py:59
  78.3 0.0 copy-done.2
  78.3 0.4 fusion.4
  78.7 0.1 copy.39
  78.8 0.1 copy.40
  78.9 0.0 copy-start.3
  78.9 0.0 copy-start.5
  79.0 0.1 broadcast_in_dim.41
  79.0 12.8 %all_to_all.35 = bf16[8,256,128]{2,1,0:T(8,128)(2,1)S(1)} all-to-all(bf16[8,256,128]{2,1,0:T(8,128)(2,1)S(1)} %broadcast_in_dim.41), channel_id=1, replica_groups=mesh['row'=64,'rep'=8] {'rep'}, dimensions={0} | all-to-all | bytes 1048576 | tf_op jit(solution)/shard_map/all_to_all | solution.py:17
  91.8 0.1 reduce_sum.40
  91.9 0.0 copy-done
  91.9 0.0 copy-done.3
  91.9 0.0 copy-done.5
  92.0 0.9 convert_reduce_fusion.1
  92.8 0.1 fusion.21
  93.0 20.2 %all_to_all.36 = f32[64,1,128]{2,1,0:T(1,128)S(1)} all-to-all(f32[64,1,128]{2,1,0:T(1,128)S(1)} %bitcast.81), channel_id=1, replica_groups=mesh['row'=64,'rep'=8] {'row'}, dimensions={0} | all-to-all | bytes 65536 | tf_op jit(solution)/shard_map/all_to_all | solution.py:10
  113.2 0.1 reduce_sum.42
  113.3 18.5 %all_to_all.37 = f32[64,1,128]{2,1,0:T(1,128)S(1)} all-to-all(f32[64,1,128]{2,1,0:T(1,128)S(1)} %broadcast_in_dim.43), channel_id=1, replica_groups=mesh['row'=64,'rep'=8] {'row'}, dimensions={0} | all-to-all | bytes 65536 | tf_op jit(solution)/shard_map/all_to_all | solution.py:17
  131.8 0.5 slice_bitcast_fusion
  132.4 0.6 slice.23
  (14 shorter events, 0.2 us)
Async XLA Ops:
  0.6 91.3 %copy-start = (bf16[128,32]{0,1:T(8,128)(2,1)S(1)}, bf16[128,32]{0,1:T(8,128)(2,1)}, u32[]{:S(2)}) copy-start(bf16[128,32]{0,1:T(8,128)(2,1)} %param.13) | copy-start | bytes 24580
  2.9 20.2 %copy-start.1 = (s32[2,8]{1,0:T(2,128)S(1)}, s32[2,8]{1,0:T(2,128)}, u32[]{:S(2)}) copy-start(s32[2,8]{1,0:T(2,128)} %param.10) | copy-start | bytes 196
  4.5 52.8 %all-to-all-start = ((bf16[64,2,2176]{2,1,0:T(2,128)(2,1)}), bf16[64,2,2176]{2,1,0:T(2,128)(2,1)S(1)}, u32[]{:S(2)}, u32[]{:S(2)}) async-start(bf16[64,2,2176]{2,1,0:T(2,128)(2,1)} %reshape.116), calls=%async_computation | async-start | bytes 1114112 | tf_op jit(solution)/shard_map/all_to_all | solution.py:39
  63.6 5.8 %copy-start.4 = (s32[2]{0:T(128)S(1)}, s32[2]{0:T(128)}, u32[]{:S(2)}) copy-start(s32[2]{0:T(128)} %param.11) | copy-start | bytes 28
  63.6 14.7 %copy-start.2 = (bf16[2,8,128,128]{3,2,1,0:T(8,128)(2,1)S(1)}, bf16[2,8,128,128]{3,2,1,0:T(8,128)(2,1)}, u32[]{:S(2)}) copy-start(bf16[2,8,128,128]{3,2,1,0:T(8,128)(2,1)} %param.12) | copy-start | bytes 1572868
  64.5 13.8 %all-to-all-start.1 = ((bf16[8,2,8,16,128]{4,3,2,1,0:T(8,128)(2,1)}), bf16[8,2,8,16,128]{4,3,2,1,0:T(8,128)(2,1)S(1)}, u32[]{:S(2)}, u32[]{:S(2)}) async-start(bf16[8,2,8,16,128]{4,3,2,1,0:T(8,128)(2,1)} %copy.37), calls=%async_computation.1 | async-start | bytes 1048576 | tf_op jit(solution)/shard_map/all_to_all | solution.py:59
  78.9 13.0 %copy-start.3 = (bf16[256,32]{0,1:T(8,128)(2,1)S(1)}, bf16[256,32]{0,1:T(8,128)(2,1)}, u32[]{:S(2)}) copy-start(bf16[256,32]{0,1:T(8,128)(2,1)} %param.15) | copy-start | bytes 49156
  78.9 13.0 %copy-start.5 = (f32[32]{0:T(128)S(1)}, f32[32]{0:T(128)}, u32[]{:S(2)}) copy-start(f32[32]{0:T(128)} %param.14) | copy-start | bytes 388
